TPU v7x, 256 devices: a whole 4x4x8 slice. The times are simulated.
256 devices in a mesh: seq: 64 (over x, z, core), head: 4 (over y).
Axes of the slice: x: 4, y: 4, z: 8, core: 2. Of those that a mesh axis runs over, the one named last changes fastest.
Arguments:
- query_rows: bfloat16 [65536, 4, 128], P(('seq', 'head')), may hold values from -5 to 5
- key_rows: bfloat16 [65536, 4, 128], P(('seq', 'head')), may hold values from -5 to 5
- value_rows: bfloat16 [65536, 4, 128], P(('seq', 'head')), may hold values from -6 to 6
- grad_rows: bfloat16 [65536, 4, 128], P(('seq', 'head')), may hold values from -6 to 6
- assignment: int32 [65536, 4], P(('seq', 'head')), may hold values from 0 to 63, as said below
- position: int32 [65536, 4], P(('seq', 'head')), may hold values from 0 to 1023, as said below
Outputs:
- attended: bfloat16 [65536, 4, 128], P(('seq', 'head'))
- grad_query: bfloat16 [65536, 4, 128], P(('seq', 'head'))
- grad_key: bfloat16 [65536, 4, 128], P(('seq', 'head'))
- grad_value: bfloat16 [65536, 4, 128], P(('seq', 'head'))
Inputs may be any that keep to these rules, and one draw needn't show every extreme that they name: `assignment`: in each head every cluster holds exactly 1024 tokens. The 256 tokens of one device send at most 6 tokens of one head to one cluster, and exactly 6 for some device, head and cluster in every draw. `position`: within each head and cluster the 1024 tokens have the places 0 to 1023, each once.
All inputs are finite; a program needn't handle non-finite values.
Results may differ from a plain program's by a relative error of at most 0.025.
Values may be sent and summed in bfloat16 or wider, within the bound.
No kernel may reach another device: no remote copies, remote signals or barrier semaphores. Data moves between devices by JAX's collectives and lax.ppermute only.
A program may use at most 64 MiB of HBM per device.

v0:
```python
import math

import jax
import jax.numpy as jnp
from jax import lax
from jax.sharding import PartitionSpec as P


def split_up(x, dim, devices):
    dims = x.shape
    parts = x.reshape(*dims[:dim], devices, dims[dim] // devices, *dims[dim + 1 :])
    return jnp.moveaxis(parts, dim, 0)


def in_order(parts, dim):
    dims = list(parts.shape[1:])
    dims[dim] *= parts.shape[0]
    return jnp.moveaxis(parts, 0, dim).reshape(dims)


def joined_exchange(x, axis, axes, splits, concats):
    sizes = [lax.axis_size(a) for a in axes]
    parts = split_up(x, splits[0], sizes[0])
    parts = jnp.moveaxis(split_up(parts, splits[1] + 1, sizes[1]), 0, 1)
    inside = parts.shape[2:]
    parts = parts.reshape(-1, *inside)
    parts = lax.all_to_all(parts, axis, split_axis=0, concat_axis=0, tiled=True)
    parts = in_order(parts.reshape(*sizes, *inside), concats[0] + 1)
    return in_order(parts, concats[1])


def cluster_slots(assign_cols, clusters, capacity):
    row_count, group_count = assign_cols.shape
    hits = assign_cols[:, :, None] == jnp.arange(clusters, dtype=jnp.int32)[None, None, :]
    onehot = hits.astype(jnp.bfloat16).reshape(row_count, group_count * clusters)
    lower = (
        lax.broadcasted_iota(jnp.int32, (row_count, row_count), 1)
        < lax.broadcasted_iota(jnp.int32, (row_count, row_count), 0)
    ).astype(jnp.bfloat16)
    earlier = jnp.dot(lower, onehot, preferred_element_type=jnp.float32).reshape(
        row_count, group_count, clusters
    )
    within = jnp.sum(jnp.where(hits, earlier, 0.0), axis=2).astype(jnp.int32)
    return assign_cols * capacity + within


def pack_slots(group_rows, group_slot, group_place, slot_count, empty_place):
    slot_ids = jnp.arange(slot_count, dtype=jnp.int32)
    hits = slot_ids[None, :, None] == group_slot[:, None, :]
    packed = jnp.einsum(
        "gsr,grf->gsf", hits.astype(jnp.bfloat16), group_rows, preferred_element_type=jnp.float32
    ).astype(jnp.bfloat16)
    filled = jnp.any(hits, axis=2)
    places = jnp.where(
        filled, jnp.sum(jnp.where(hits, group_place[:, None, :], 0), axis=2), empty_place
    )
    return (packed, places)


def place_tables(flat_place, cluster_len, block_rows):
    tables = []
    for block_index in range(cluster_len // block_rows):
        row_ids = block_index * block_rows + jnp.arange(block_rows, dtype=jnp.int32)
        tables.append((row_ids[:, None] == flat_place[None, :]).astype(jnp.bfloat16))
    return tables


def slots_to_order(tables, arrived_flat):
    return jnp.concatenate(
        [
            jnp.dot(table, arrived_flat, preferred_element_type=jnp.float32).astype(jnp.bfloat16)
            for table in tables
        ],
        axis=0,
    )


def order_to_slots(tables, result_flat, block_rows):
    total = None
    for block_index, table in enumerate(tables):
        piece = result_flat[block_index * block_rows : (block_index + 1) * block_rows]
        term = jnp.einsum("la,lf->af", table, piece, preferred_element_type=jnp.float32)
        total = term if total is None else total + term
    return total.astype(jnp.bfloat16)


def slots_to_rows(returned, local_slot):
    head_count = returned.shape[0]
    flat_rows = returned.reshape(head_count, -1, returned.shape[-1])
    slot_ids = jnp.arange(flat_rows.shape[1], dtype=jnp.int32)
    hits = (local_slot[:, :, None] == slot_ids[None, None, :]).astype(jnp.bfloat16)
    return jnp.einsum("rhs,hsf->rhf", hits, flat_rows, preferred_element_type=jnp.float32).astype(
        jnp.bfloat16
    )


def masked_scores(query_part, key_part, row_start, score_scale):
    scores = (
        jnp.einsum("qd,kd->qk", query_part, key_part, preferred_element_type=jnp.float32)
        * score_scale
    )
    row_ids = row_start + lax.broadcasted_iota(jnp.int32, scores.shape, 0)
    col_ids = lax.broadcasted_iota(jnp.int32, scores.shape, 1)
    return jnp.where(col_ids <= row_ids, scores, -jnp.inf)


def forward_pass(query_block, key_block, value_block, block_rows, score_scale):
    pieces, row_tops, row_totals = ([], [], [])
    for block_index in range(query_block.shape[0] // block_rows):
        row_start = block_index * block_rows
        finish = row_start + block_rows
        scores = masked_scores(
            query_block[row_start:finish], key_block[:finish], row_start, score_scale
        )
        row_top = jnp.max(scores, axis=1, keepdims=True)
        weights = jnp.exp(scores - row_top)
        row_total = jnp.sum(weights, axis=1, keepdims=True)
        probs_low = (weights / row_total).astype(jnp.bfloat16)
        pieces.append(
            jnp.dot(probs_low, value_block[:finish], preferred_element_type=jnp.float32).astype(
                jnp.bfloat16
            )
        )
        row_tops.append(row_top)
        row_totals.append(row_total)
    return (jnp.concatenate(pieces, axis=0), row_tops, row_totals)


def backward_pass(
    query_block,
    key_block,
    value_block,
    grad_block,
    attended_block,
    row_tops,
    row_totals,
    block_rows,
    score_scale,
):
    row_count, head_width = query_block.shape
    grad_key_sum = jnp.zeros((row_count, head_width), jnp.float32)
    grad_value_sum = jnp.zeros((row_count, head_width), jnp.float32)
    query_parts = []
    for block_index in range(row_count // block_rows):
        row_start = block_index * block_rows
        finish = row_start + block_rows
        scores = masked_scores(
            query_block[row_start:finish], key_block[:finish], row_start, score_scale
        )
        probabilities = jnp.exp(scores - row_tops[block_index]) / row_totals[block_index]
        probs_low = probabilities.astype(jnp.bfloat16)
        grad_part = grad_block[row_start:finish]
        grad_prob = jnp.einsum(
            "qd,kd->qk", grad_part, value_block[:finish], preferred_element_type=jnp.float32
        )
        row_delta = jnp.sum(
            grad_part.astype(jnp.float32) * attended_block[row_start:finish].astype(jnp.float32),
            axis=1,
            keepdims=True,
        )
        grad_score = (probabilities * (grad_prob - row_delta)).astype(jnp.bfloat16)
        query_parts.append(
            (
                jnp.dot(grad_score, key_block[:finish], preferred_element_type=jnp.float32)
                * score_scale
            ).astype(jnp.bfloat16)
        )
        key_term = jnp.einsum(
            "qk,qd->kd",
            grad_score,
            query_block[row_start:finish],
            preferred_element_type=jnp.float32,
        )
        value_term = jnp.einsum(
            "qk,qd->kd", probs_low, grad_part, preferred_element_type=jnp.float32
        )
        grad_key_sum = grad_key_sum + jnp.pad(key_term, ((0, row_count - finish), (0, 0)))
        grad_value_sum = grad_value_sum + jnp.pad(value_term, ((0, row_count - finish), (0, 0)))
    grad_query_block = jnp.concatenate(query_parts, axis=0)
    grad_key_block = (grad_key_sum * score_scale).astype(jnp.bfloat16)
    grad_value_block = grad_value_sum.astype(jnp.bfloat16)
    return jnp.stack((grad_query_block, grad_key_block, grad_value_block), axis=1)


def shards(query_rows, key_rows, value_rows, grad_rows, assignment, position):
    sub_rows, head_count, head_width = query_rows.shape
    clusters = lax.axis_size("seq")
    cluster_len = sub_rows * lax.axis_size("head")
    capacity = 3 * sub_rows // (2 * clusters)
    slot_count = clusters * capacity
    stacked = jnp.stack((query_rows, key_rows, value_rows, grad_rows), axis=2)
    local_slot = cluster_slots(assignment, clusters, capacity)
    group_rows = jnp.transpose(stacked.reshape(sub_rows, head_count, 4 * head_width), (1, 0, 2))
    packed, places = pack_slots(group_rows, local_slot.T, position.T, slot_count, cluster_len)
    arrived, arrived_place = (
        joined_exchange(
            packed.reshape(head_count, clusters, capacity, 4, head_width),
            ("seq", "head"),
            ("seq", "head"),
            (1, 0),
            (1, 0),
        ),
        joined_exchange(
            places.reshape(head_count, clusters, capacity),
            ("seq", "head"),
            ("seq", "head"),
            (1, 0),
            (1, 0),
        ),
    )
    lead_shape = arrived_place.shape
    flat_place = arrived_place.reshape(-1)
    block_rows = min(512, cluster_len)
    tables = place_tables(flat_place, cluster_len, block_rows)
    ordered = slots_to_order(tables, arrived.reshape(-1, 4 * head_width)).reshape(
        cluster_len, 4, head_width
    )
    query_block = ordered[:, 0]
    key_block = ordered[:, 1]
    value_block = ordered[:, 2]
    grad_block = ordered[:, 3]
    score_scale = 1.0 / math.sqrt(head_width)
    attended_block, row_tops, row_totals = forward_pass(
        query_block, key_block, value_block, block_rows, score_scale
    )
    grads_block = backward_pass(
        query_block,
        key_block,
        value_block,
        grad_block,
        attended_block,
        row_tops,
        row_totals,
        block_rows,
        score_scale,
    )
    combined = jnp.concatenate((attended_block[:, None], grads_block), axis=1).reshape(
        cluster_len, 4 * head_width
    )
    all_slots = order_to_slots(tables, combined, block_rows).reshape(lead_shape + (4 * head_width,))
    returned_all = joined_exchange(all_slots, ("seq", "head"), ("seq", "head"), (1, 0), (1, 0))
    everything = slots_to_rows(returned_all, local_slot).reshape(
        sub_rows, head_count, 4, head_width
    )
    return (everything[:, :, 0], everything[:, :, 1], everything[:, :, 2], everything[:, :, 3])


def solution(mesh):
    return jax.shard_map(
        shards,
        mesh=mesh,
        in_specs=(
            P(("seq", "head"), None, None),
            P(("seq", "head"), None, None),
            P(("seq", "head"), None, None),
            P(("seq", "head"), None, None),
            P(("seq", "head"), None),
            P(("seq", "head"), None),
        ),
        out_specs=(
            P(("seq", "head"), None, None),
            P(("seq", "head"), None, None),
            P(("seq", "head"), None, None),
            P(("seq", "head"), None, None),
        ),
        check_vma=False,
    )
```

profile of v0, /device:TPU:1, one launch (start us, length us, event | category | flops | bytes accessed | tf_op | source)
XLA Modules:
  0.0 171.3 jit_solution(12516590646175196772)
XLA Ops:
  0.7 0.8 bitcast_compare_fusion
  1.5 0.9 fusion.43
  2.5 0.7 convert_add_fusion
  3.1 0.3 fusion.17
  3.5 1.0 select_reduce_fusion
  4.6 0.7 copy.145
  5.3 15.6 %all-to-all-start = ((s32[256,1,1,6]{3,2,1,0:T(1,128)}), s32[256,1,1,6]{3,2,1,0:T(1,128)S(1)}, u32[]{:S(2)}, u32[]{:S(2)}) async-start(s32[256,1,1,6]{3,2,1,0:T(1,128)} %bitcast.7), calls=%async_computation | async-start | bytes 262144 | tf_op jit(solution)/shard_map/all_to_all | solution.py:27
  21.0 2.1 %pad_maximum_fusion = bf16[256,4,4,128]{3,1,0,2:T(4,128)(2,1)S(1)} fusion(bf16[256,4,1,128]{3,1,0,2:T(4,128)(2,1)} %bitcast.144, bf16[256,4,1,128]{3,1,0,2:T(4,128)(2,1)} %bitcast.145, bf16[256,4,1,128]{3,1,0,2:T(4,128)(2,1)} %bitcast.146, bf16[256,4,1,128]{3,1,0,2:T(4,128)(2,1)} %bitcast.147), kind=kLoop, calls=%fused_computation.56 | loop fusion | flops 1572864 | bytes 2097152 | tf_op jit(solution)/shard_map/stack | solution.py:191
  23.1 0.8 copy.112
  24.0 0.4 reshape.75
  24.4 0.6 convolution_convert_fusion
  25.0 0.4 reshape_reshape.17
  25.4 1.2 copy.113
  26.6 2.4 %copy.114 = bf16[256,1,1,6,4,128]{5,4,3,2,1,0:T(4,128)(2,1)} copy(bf16[256,1,1,6,4,128]{5,0,4,3,2,1:T(8,128)(2,1)S(1)} %bitcast.129) | data formatting | bytes 3145728 | tf_op jit(solution)/shard_map/reshape;reshape | solution.py:26
  29.0 4.7 %all-to-all-done = s32[256,1,1,6]{3,2,1,0:T(1,128)S(1)} async-done(((s32[256,1,1,6]{3,2,1,0:T(1,128)}), s32[256,1,1,6]{3,2,1,0:T(1,128)S(1)}, u32[]{:S(2)}, u32[]{:S(2)}) %all-to-all-start) | async-done | bytes 6176 | tf_op jit(solution)/shard_map/all_to_all | solution.py:27
  33.7 9.0 %all-to-all-start.1 = ((bf16[256,1,1,6,4,128]{5,4,3,2,1,0:T(4,128)(2,1)}), bf16[256,1,1,6,4,128]{5,4,3,2,1,0:T(4,128)(2,1)S(1)}, u32[]{:S(2)}, u32[]{:S(2)}) async-start(bf16[256,1,1,6,4,128]{5,4,3,2,1,0:T(4,128)(2,1)} %copy.114), calls=%async_computation.1 | async-start | bytes 3145728 | tf_op jit(solution)/shard_map/all_to_all | solution.py:27
  42.8 0.6 copy.146
  43.4 0.6 copy.111
  44.1 42.3 %all-to-all-done.1 = bf16[256,1,1,6,4,128]{5,4,3,2,1,0:T(4,128)(2,1)S(1)} async-done(((bf16[256,1,1,6,4,128]{5,4,3,2,1,0:T(4,128)(2,1)}), bf16[256,1,1,6,4,128]{5,4,3,2,1,0:T(4,128)(2,1)S(1)}, u32[]{:S(2)}, u32[]{:S(2)}) %all-to-all-start.1) | async-done | bytes 1572896 | tf_op jit(solution)/shard_map/all_to_all | solution.py:27
  86.4 0.5 copy.115
  87.0 1.0 fusion.28
  88.0 1.0 fusion.31
  89.4 0.9 fusion.59
  90.3 1.1 fusion.58
  91.4 0.3 fusion.60
  92.1 0.3 fusion.55
  92.4 0.4 multiply_reduce_fusion.1
  92.9 0.3 fusion.27
  93.2 0.3 fusion.41
  93.9 0.6 fusion.61
  94.4 0.5 fusion.6
  95.0 0.5 fusion.5
  95.5 0.5 fusion.40
  96.0 0.5 multiply_reduce_fusion
  96.5 0.5 multiply_convert_fusion
  97.0 0.4 fusion.42
  97.4 0.5 fusion.39
  98.6 1.0 fusion.7
  99.6 2.4 %fusion.4 = bf16[1536,512]{1,0:T(8,128)(2,1)} fusion(f32[1536,512]{1,0:T(8,128)S(1)} %fusion.7, bf16[512,512]{0,1:T(8,128)(2,1)S(1)} %bitcast.136, s32[1536]{0:T(1024)S(1)} %eq.88, s32[512]{0:T(512)S(1)} %iota_add_fusion), kind=kOutput, calls=%fused_computation.7 | convolution fusion | flops 808452096 | bytes 5251072 | tf_op jit(solution)/shard_map/la,lf->af/dot_general | solution.py:82
  102.0 2.5 %reshape_reshape.19 = bf16[4,64,1,6,512]{4,3,1,0,2:T(8,128)(2,1)S(1)} reshape(bf16[1536,512]{1,0:T(8,128)(2,1)} %fusion.4) | data formatting | bytes 3145728 | tf_op jit(solution)/shard_map/reshape;reshape | solution.py:11
  104.7 60.5 %all_to_all.15 = bf16[256,1,1,6,512]{4,3,2,1,0:T(8,128)(2,1)S(1)} all-to-all(bf16[256,1,1,6,512]{4,3,2,1,0:T(8,128)(2,1)S(1)} %bitcast.127), channel_id=1, replica_groups=mesh['seq'=64,'head'=4] {'seq','head'}, dimensions={0} | all-to-all | bytes 3145728 | tf_op jit(solution)/shard_map/all_to_all | solution.py:27
  165.2 0.8 copy.221
  166.1 0.5 copy.134
  166.6 1.1 fusion.20
  167.8 0.9 copy.162
  168.7 0.9 copy.161
  169.5 0.9 copy.160
  170.4 0.9 copy.159
  (18 shorter events, 2.4 us)
Async XLA Ops:
  5.3 28.4 %all-to-all-start = ((s32[256,1,1,6]{3,2,1,0:T(1,128)}), s32[256,1,1,6]{3,2,1,0:T(1,128)S(1)}, u32[]{:S(2)}, u32[]{:S(2)}) async-start(s32[256,1,1,6]{3,2,1,0:T(1,128)} %bitcast.7), calls=%async_computation | async-start | bytes 262144 | tf_op jit(solution)/shard_map/all_to_all | solution.py:27
  33.7 52.7 %all-to-all-start.1 = ((bf16[256,1,1,6,4,128]{5,4,3,2,1,0:T(4,128)(2,1)}), bf16[256,1,1,6,4,128]{5,4,3,2,1,0:T(4,128)(2,1)S(1)}, u32[]{:S(2)}, u32[]{:S(2)}) async-start(bf16[256,1,1,6,4,128]{5,4,3,2,1,0:T(4,128)(2,1)} %copy.114), calls=%async_computation.1 | async-start | bytes 3145728 | tf_op jit(solution)/shard_map/all_to_all | solution.py:27
where the time goes:
time: 172 us; the launch traced here: 171 us
  blocking collectives  60.5 us (35%)
  waiting for transfers between devices  47 us (27%)
  starting transfers between devices  24.7 us (14%)
  local copies, waits for them, and re-layouts  18.5 us (11%)
  matrix products  13.1 us (8%)
  other arithmetic  6.53 us (4%)
    all_to_all x1, blocking collectives, joined_exchange(): parts = lax.all_to_all(parts, axis, split_axis=0, concat_axis=0, tiled=True)  60.5 us
    all_to_all x2, waiting for transfers between devices, joined_exchange(): parts = lax.all_to_all(parts, axis, split_axis=0, concat_axis=0, tiled=True)  47 us
    all_to_all x2, starting transfers between devices, joined_exchange(): parts = lax.all_to_all(parts, axis, split_axis=0, concat_axis=0, tiled=True)  24.7 us
    another operation x3, local copies, waits for them, and re-layouts, split_up(): x.reshape(*dims[:dim], devices, dims[dim] // devices, *dims[dim + 1:])  4.11 us
    unnamed x4, local copies, waits for them, and re-layouts  3.47 us
  transfers between devices with their start and end apart: 2, of which 2 were waited for; matrix products, arithmetic and copies ran while one was open for 5% of the time, Pallas kernels for 0%

commit v1 on v0

--- a/solution.py
+++ b/solution.py
@@ -188,33 +188,35 @@
     cluster_len = sub_rows * lax.axis_size("head")
     capacity = 3 * sub_rows // (2 * clusters)
     slot_count = clusters * capacity
+    devices = clusters * head_count
     stacked = jnp.stack((query_rows, key_rows, value_rows, grad_rows), axis=2)
     local_slot = cluster_slots(assignment, clusters, capacity)
     group_rows = jnp.transpose(stacked.reshape(sub_rows, head_count, 4 * head_width), (1, 0, 2))
     packed, places = pack_slots(group_rows, local_slot.T, position.T, slot_count, cluster_len)
-    arrived, arrived_place = (
-        joined_exchange(
-            packed.reshape(head_count, clusters, capacity, 4, head_width),
-            ("seq", "head"),
-            ("seq", "head"),
-            (1, 0),
-            (1, 0),
-        ),
-        joined_exchange(
-            places.reshape(head_count, clusters, capacity),
-            ("seq", "head"),
-            ("seq", "head"),
-            (1, 0),
-            (1, 0),
-        ),
-    )
-    lead_shape = arrived_place.shape
-    flat_place = arrived_place.reshape(-1)
+    packed = jnp.transpose(
+        packed.reshape(head_count, clusters, capacity, 4 * head_width), (1, 0, 2, 3)
+    ).reshape(devices, capacity * 4, head_width)
+    places = jnp.transpose(places.reshape(head_count, clusters, capacity), (1, 0, 2)).reshape(
+        devices, capacity
+    )
+    coded = jnp.concatenate((places // 32, places % 32), axis=1).astype(jnp.bfloat16)
+    coded = jnp.pad(coded, ((0, 0), (0, 2 * head_width - 2 * capacity))).reshape(
+        devices, 2, head_width
+    )
+    payload = jnp.concatenate((packed, coded), axis=1)
+    rows = payload.shape[1]
+    payload = payload.reshape(devices, rows // 2, 2, head_width)
+    arrived = lax.all_to_all(payload, ("seq", "head"), 0, 0, tiled=True).reshape(
+        devices, rows, head_width
+    )
+    arrived_data = arrived[:, : capacity * 4].reshape(devices * capacity, 4 * head_width)
+    arrived_code = arrived[:, capacity * 4].astype(jnp.float32)
+    flat_place = (
+        arrived_code[:, :capacity] * 32.0 + arrived_code[:, capacity : 2 * capacity]
+    ).astype(jnp.int32).reshape(-1)
     block_rows = min(512, cluster_len)
     tables = place_tables(flat_place, cluster_len, block_rows)
-    ordered = slots_to_order(tables, arrived.reshape(-1, 4 * head_width)).reshape(
-        cluster_len, 4, head_width
-    )
+    ordered = slots_to_order(tables, arrived_data).reshape(cluster_len, 4, head_width)
     query_block = ordered[:, 0]
     key_block = ordered[:, 1]
     value_block = ordered[:, 2]
@@ -237,11 +239,14 @@
     combined = jnp.concatenate((attended_block[:, None], grads_block), axis=1).reshape(
         cluster_len, 4 * head_width
     )
-    all_slots = order_to_slots(tables, combined, block_rows).reshape(lead_shape + (4 * head_width,))
-    returned_all = joined_exchange(all_slots, ("seq", "head"), ("seq", "head"), (1, 0), (1, 0))
-    everything = slots_to_rows(returned_all, local_slot).reshape(
-        sub_rows, head_count, 4, head_width
-    )
+    all_slots = order_to_slots(tables, combined, block_rows).reshape(
+        devices, capacity, 4, head_width
+    )
+    returned = lax.all_to_all(all_slots, ("seq", "head"), 0, 0, tiled=True)
+    returned = jnp.transpose(
+        returned.reshape(clusters, head_count, capacity, 4 * head_width), (1, 0, 2, 3)
+    ).reshape(head_count, slot_count, 4 * head_width)
+    everything = slots_to_rows(returned, local_slot).reshape(sub_rows, head_count, 4, head_width)
     return (everything[:, :, 0], everything[:, :, 1], everything[:, :, 2], everything[:, :, 3])
 
 

time: 172 us -> 154 us (0.90)
  blocking collectives: 60.5 us -> 49.4 us
  starting transfers between devices: 24.7 us -> 15.7 us
  local copies, waits for them, and re-layouts: 18.5 us -> 20.8 us
  other arithmetic: 6.53 us -> 8.5 us
    all_to_all x1, blocking collectives: 60.5 us -> 49.4 us  [shards(): returned = lax.all_to_all(all_slots, ('seq', 'head'), 0, 0, tiled=True)]
    all_to_all x2 -> x1, starting transfers between devices: 24.7 us -> 15.7 us  [shards(): lax.all_to_all(payload, ('seq', 'head'), 0, 0, tiled=True)]
    another operation x6 -> x0, local copies, waits for them, and re-layouts: 7.46 us -> none  [the longest x3 4.11 us: split_up(): x.reshape(*dims[:dim], devices, dims[dim] // devices, *dims[dim + 1:])]
    reshape x4 -> x8, local copies, waits for them, and re-layouts: 2.25 us -> 7.45 us  [the longest x1 2.94 us: shards(): payload = payload.reshape(devices, rows // 2, 2, head_width)]
    concatenate x0 -> x2, other arithmetic: none -> 1.85 us  [the longest x1 1.83 us: shards(): payload = jnp.concatenate((packed, coded), axis=1)]
    all_to_all x2 -> x1, waiting for transfers between devices: 47 us -> 46.5 us  [shards(): lax.all_to_all(payload, ('seq', 'head'), 0, 0, tiled=True)]
  transfers between devices with their start and end apart: 2 -> 1, of which waited for: 2 -> 1; matrix products, arithmetic and copies ran while one was open for 5% -> 0% of each run, Pallas kernels for 0% -> 0%
where the time goes in v1:
time: 154 us
  blocking collectives  49.4 us (32%)
  waiting for transfers between devices  46.5 us (30%)
  local copies, waits for them, and re-layouts  20.8 us (14%)
  starting transfers between devices  15.7 us (10%)
  matrix products  11.9 us (8%)
  other arithmetic  8.5 us (6%)
    all_to_all x1, blocking collectives, shards(): returned = lax.all_to_all(all_slots, ('seq', 'head'), 0, 0, tiled=True)  49.4 us
    all_to_all x1, waiting for transfers between devices, shards(): lax.all_to_all(payload, ('seq', 'head'), 0, 0, tiled=True)  46.5 us
    all_to_all x1, starting transfers between devices, shards(): lax.all_to_all(payload, ('seq', 'head'), 0, 0, tiled=True)  15.7 us
    unnamed x4, local copies, waits for them, and re-layouts  3.47 us
  transfers between devices with their start and end apart: 1, of which 1 were waited for; matrix products, arithmetic and copies ran while one was open for 0% of the time, Pallas kernels for 0%

profile of v1, /device:TPU:1, one launch (start us, length us, event | category | flops | bytes accessed | tf_op | source)
XLA Modules:
  0.0 153.7 jit_solution(470445739437470128)
XLA Ops:
  0.7 0.8 bitcast_compare_fusion
  1.5 0.9 fusion.35
  2.5 0.7 convert_add_fusion
  3.5 1.0 select_reduce_fusion
  4.6 0.6 copy.81
  5.5 2.1 %pad_maximum_fusion.1 = bf16[256,4,4,128]{3,1,0,2:T(4,128)(2,1)S(1)} fusion(bf16[256,4,1,128]{3,1,0,2:T(4,128)(2,1)} %bitcast.128, bf16[256,4,1,128]{3,1,0,2:T(4,128)(2,1)} %bitcast.129, bf16[256,4,1,128]{3,1,0,2:T(4,128)(2,1)} %bitcast.130, bf16[256,4,1,128]{3,1,0,2:T(4,128)(2,1)} %bitcast.131), kind=kLoop, calls=%fused_computation.52 | loop fusion | flops 1572864 | bytes 2097152 | tf_op jit(solution)/shard_map/stack | solution.py:192
  7.7 0.8 copy.78
  8.5 0.4 reshape.83
  8.9 0.6 convolution_convert_fusion
  9.5 1.2 copy.79
  10.7 0.6 copy.80
  11.3 1.9 %reshape.85 = bf16[256,24,128]{2,1,0:T(8,128)(2,1)} reshape(bf16[64,4,6,512]{3,2,1,0:T(8,128)(2,1)S(1)} %copy.80) | data formatting | bytes 3145728 | tf_op jit(solution)/shard_map/reshape | solution.py:198
  13.2 1.8 %pad_maximum_fusion = bf16[256,26,128]{2,1,0:T(8,128)(2,1)S(1)} fusion(bf16[256,2,128]{2,1,0:T(2,128)(2,1)S(1)} %copy.114, bf16[256,24,128]{2,1,0:T(8,128)(2,1)} %reshape.85), kind=kLoop, calls=%fused_computation.8 | loop fusion | flops 3407872 | bytes 3407872 | tf_op jit(solution)/shard_map/concatenate | solution.py:206
  15.1 0.7 copy.83
  15.7 2.9 %copy.84 = bf16[256,13,2,128]{3,2,1,0:T(2,128)(2,1)} copy(bf16[256,13,2,128]{3,0,2,1:T(8,128)(2,1)S(1)} %bitcast.113) | data formatting | bytes 3407872 | tf_op jit(solution)/shard_map/reshape | solution.py:208
  18.7 15.7 %all-to-all-start = ((bf16[256,13,2,128]{3,2,1,0:T(2,128)(2,1)}), bf16[256,13,2,128]{3,2,1,0:T(2,128)(2,1)S(1)}, u32[]{:S(2)}, u32[]{:S(2)}) async-start(bf16[256,13,2,128]{3,2,1,0:T(2,128)(2,1)} %copy.84), calls=%async_computation | async-start | bytes 3407872 | tf_op jit(solution)/shard_map/all_to_all | solution.py:209
  34.4 46.5 %all-to-all-done = bf16[256,13,2,128]{3,2,1,0:T(2,128)(2,1)S(1)} async-done(((bf16[256,13,2,128]{3,2,1,0:T(2,128)(2,1)}), bf16[256,13,2,128]{3,2,1,0:T(2,128)(2,1)S(1)}, u32[]{:S(2)}, u32[]{:S(2)}) %all-to-all-start) | async-done | bytes 1703968 | tf_op jit(solution)/shard_map/all_to_all | solution.py:209
  80.8 0.4 copy.85
  81.3 1.0 copy.86
  82.3 1.0 reshape.90
  83.6 1.0 fusion.24
  84.6 1.0 fusion.25
  86.0 0.9 fusion.60
  86.9 1.1 fusion.59
  88.0 0.3 fusion.61
  89.0 0.4 multiply_reduce_fusion.1
  89.5 0.3 fusion.23
  89.8 0.3 fusion.33
  90.5 0.6 fusion.62
  91.0 0.5 fusion.6
  91.6 0.5 fusion.5
  92.1 0.5 fusion.32
  92.6 0.5 multiply_reduce_fusion
  93.1 0.5 multiply_convert_fusion
  93.5 0.4 fusion.34
  94.0 0.5 fusion.31
  95.2 1.0 fusion.7
  96.2 1.2 fusion.4
  97.5 0.4 reshape.92
  97.9 49.4 %all_to_all.10 = bf16[256,6,4,128]{3,2,1,0:T(4,128)(2,1)S(1)} all-to-all(bf16[256,6,4,128]{3,2,1,0:T(4,128)(2,1)S(1)} %reshape.92), channel_id=1, replica_groups=mesh['seq'=64,'head'=4] {'seq','head'}, dimensions={0} | all-to-all | bytes 3145728 | tf_op jit(solution)/shard_map/all_to_all | solution.py:245
  147.3 0.5 copy.102
  147.8 0.6 reshape.93
  148.5 0.5 copy.103
  149.0 1.1 fusion.18
  150.2 0.9 copy.126
  151.1 0.9 copy.125
  152.0 0.9 copy.124
  152.8 0.9 copy.123
  (26 shorter events, 3.2 us)
Async XLA Ops:
  18.7 62.1 %all-to-all-start = ((bf16[256,13,2,128]{3,2,1,0:T(2,128)(2,1)}), bf16[256,13,2,128]{3,2,1,0:T(2,128)(2,1)S(1)}, u32[]{:S(2)}, u32[]{:S(2)}) async-start(bf16[256,13,2,128]{3,2,1,0:T(2,128)(2,1)} %copy.84), calls=%async_computation | async-start | bytes 3407872 | tf_op jit(solution)/shard_map/all_to_all | solution.py:209

commit v2 on v1

--- a/solution.py
+++ b/solution.py
@@ -189,26 +189,29 @@
     capacity = 3 * sub_rows // (2 * clusters)
     slot_count = clusters * capacity
     devices = clusters * head_count
+    order = ("head", "seq")
+    local_slot = cluster_slots(assignment, clusters, capacity)
+    slot_ids = jnp.arange(slot_count, dtype=jnp.int32)
+    hits = slot_ids[None, :, None] == local_slot.T[:, None, :]
+    hits_low = hits.astype(jnp.bfloat16)
     stacked = jnp.stack((query_rows, key_rows, value_rows, grad_rows), axis=2)
-    local_slot = cluster_slots(assignment, clusters, capacity)
-    group_rows = jnp.transpose(stacked.reshape(sub_rows, head_count, 4 * head_width), (1, 0, 2))
-    packed, places = pack_slots(group_rows, local_slot.T, position.T, slot_count, cluster_len)
-    packed = jnp.transpose(
-        packed.reshape(head_count, clusters, capacity, 4 * head_width), (1, 0, 2, 3)
-    ).reshape(devices, capacity * 4, head_width)
-    places = jnp.transpose(places.reshape(head_count, clusters, capacity), (1, 0, 2)).reshape(
-        devices, capacity
-    )
+    packed = jnp.einsum(
+        "hsr,rhaf->hsaf", hits_low, stacked, preferred_element_type=jnp.float32
+    ).astype(jnp.bfloat16)
+    places = jnp.where(
+        jnp.any(hits, axis=2),
+        jnp.sum(jnp.where(hits, position.T[:, None, :], 0), axis=2),
+        cluster_len,
+    ).reshape(devices, capacity)
     coded = jnp.concatenate((places // 32, places % 32), axis=1).astype(jnp.bfloat16)
     coded = jnp.pad(coded, ((0, 0), (0, 2 * head_width - 2 * capacity))).reshape(
-        devices, 2, head_width
-    )
-    payload = jnp.concatenate((packed, coded), axis=1)
-    rows = payload.shape[1]
-    payload = payload.reshape(devices, rows // 2, 2, head_width)
-    arrived = lax.all_to_all(payload, ("seq", "head"), 0, 0, tiled=True).reshape(
-        devices, rows, head_width
-    )
+        devices, 1, 2, head_width
+    )
+    payload = jnp.concatenate(
+        (packed.reshape(devices, capacity * 2, 2, head_width), coded), axis=1
+    )
+    rows = 2 * payload.shape[1]
+    arrived = lax.all_to_all(payload, order, 0, 0, tiled=True).reshape(devices, rows, head_width)
     arrived_data = arrived[:, : capacity * 4].reshape(devices * capacity, 4 * head_width)
     arrived_code = arrived[:, capacity * 4].astype(jnp.float32)
     flat_place = (
@@ -242,12 +245,21 @@
     all_slots = order_to_slots(tables, combined, block_rows).reshape(
         devices, capacity, 4, head_width
     )
-    returned = lax.all_to_all(all_slots, ("seq", "head"), 0, 0, tiled=True)
-    returned = jnp.transpose(
-        returned.reshape(clusters, head_count, capacity, 4 * head_width), (1, 0, 2, 3)
-    ).reshape(head_count, slot_count, 4 * head_width)
-    everything = slots_to_rows(returned, local_slot).reshape(sub_rows, head_count, 4, head_width)
-    return (everything[:, :, 0], everything[:, :, 1], everything[:, :, 2], everything[:, :, 3])
+    returned = lax.all_to_all(all_slots, order, 0, 0, tiled=True).reshape(
+        head_count, slot_count, 4, head_width
+    )
+    return tuple(
+        jnp.stack(
+            [
+                jnp.dot(
+                    hits_low[head].T, returned[head, :, member], preferred_element_type=jnp.float32
+                ).astype(jnp.bfloat16)
+                for head in range(head_count)
+            ],
+            axis=1,
+        )
+        for member in range(4)
+    )
 
 
 def solution(mesh):

time: 154 us -> 151 us (0.981)
  local copies, waits for them, and re-layouts: 20.8 us -> 14.8 us
  matrix products: 11.9 us -> 15.8 us
    reshape x5 -> x0, local copies, waits for them, and re-layouts: 6.08 us -> none  [the longest x1 2.94 us: shards(): payload = payload.reshape(devices, rows // 2, 2, head_width)]
    dot_general x2 -> x17, matrix products: 1.68 us -> 5.58 us  [the longest x16 5 us: shards(): jnp.dot(hits_low[head].T, returned[head, :, member], preferred_element_ty...]
    slice x1, local copies, waits for them, and re-layouts: 0.07 us -> 3.25 us  [shards(): returned[head, :, member]]
    another operation x2 -> x7, other arithmetic: 2.16 us -> 0.18 us  [the longest x4 0.15 us: shards(): jnp.stack([jnp.dot(hits_low[head].T, returned[head, :, member], preferred...]
    transpose x3 -> x0, local copies, waits for them, and re-layouts: 1.73 us -> none  [the longest x1 0.61 us: shards(): jnp.transpose(places.reshape(head_count, clusters, capacity), (1, 0, 2))]
    concatenate x1, other arithmetic: 1.83 us -> 3.42 us  [shards(): jnp.concatenate((packed.reshape(devices, capacity * 2, 2, head_width), co...]
    unnamed x4 -> x14, local copies, waits for them, and re-layouts: 3.47 us -> 3.65 us
where the time goes in v2:
time: 151 us
  blocking collectives  48 us (32%)
  waiting for transfers between devices  46.5 us (31%)
  matrix products  15.8 us (10%)
  starting transfers between devices  15.6 us (10%)
  local copies, waits for them, and re-layouts  14.8 us (10%)
  other arithmetic  8.99 us (6%)
    all_to_all x1, blocking collectives, shards(): lax.all_to_all(all_slots, order, 0, 0, tiled=True)  48 us
    all_to_all x1, waiting for transfers between devices, shards(): lax.all_to_all(payload, order, 0, 0, tiled=True)  46.5 us
    all_to_all x1, starting transfers between devices, shards(): lax.all_to_all(payload, order, 0, 0, tiled=True)  15.6 us
    dot_general x16, matrix products, shards(): jnp.dot(hits_low[head].T, returned[head, :, member], preferred_element_ty...  5 us
    unnamed x14, local copies, waits for them, and re-layouts  3.65 us
    concatenate x1, other arithmetic, shards(): jnp.concatenate((packed.reshape(devices, capacity * 2, 2, head_width), co...  3.42 us
    slice x1, local copies, waits for them, and re-layouts, shards(): returned[head, :, member]  3.25 us
  transfers between devices with their start and end apart: 1, of which 1 were waited for; matrix products, arithmetic and copies ran while one was open for 0% of the time, Pallas kernels for 0%

profile of v2, /device:TPU:1, one launch (start us, length us, event | category | flops | bytes accessed | tf_op | source)
XLA Modules:
  0.0 150.9 jit_solution(14431048166594893667)
XLA Ops:
  0.8 0.9 bitcast_compare_fusion
  1.6 0.9 fusion.31
  2.6 0.7 add_bitcast_fusion
  3.3 1.0 fusion.23
  4.3 1.0 select_reduce_fusion
  6.1 0.6 convolution_convert_fusion
  6.7 1.2 copy.80
  7.9 3.4 %pad_maximum_fusion = bf16[256,13,2,128]{3,2,1,0:T(2,128)(2,1)} fusion(bf16[256,1,2,128]{3,2,1,0:T(2,128)(2,1)S(1)} %copy.111, bf16[256,12,2,128]{3,2,1,0:T(2,128)(2,1)S(1)} %bitcast.209), kind=kLoop, calls=%fused_computation.14 | loop fusion | flops 851968 | bytes 3407872 | tf_op jit(solution)/shard_map/concatenate | solution.py:210
  11.3 15.6 %all-to-all-start = ((bf16[256,13,2,128]{3,2,1,0:T(2,128)(2,1)}), bf16[256,13,2,128]{3,2,1,0:T(2,128)(2,1)S(1)}, u32[]{:S(2)}, u32[]{:S(2)}) async-start(bf16[256,13,2,128]{3,2,1,0:T(2,128)(2,1)} %pad_maximum_fusion), calls=%async_computation | async-start | bytes 3407872 | tf_op jit(solution)/shard_map/all_to_all | solution.py:214
  27.0 46.5 %all-to-all-done = bf16[256,13,2,128]{3,2,1,0:T(2,128)(2,1)S(1)} async-done(((bf16[256,13,2,128]{3,2,1,0:T(2,128)(2,1)}), bf16[256,13,2,128]{3,2,1,0:T(2,128)(2,1)S(1)}, u32[]{:S(2)}, u32[]{:S(2)}) %all-to-all-start) | async-done | bytes 1703968 | tf_op jit(solution)/shard_map/all_to_all | solution.py:214
  73.4 0.4 copy.84
  73.9 1.0 copy.85
  74.9 1.0 reshape.67
  76.2 1.0 fusion.19
  77.2 1.0 fusion.20
  78.3 0.5 reshape.68
  78.8 0.9 fusion.108
  79.7 1.1 fusion.107
  80.8 0.3 fusion.109
  81.8 0.4 multiply_reduce_fusion.1
  82.2 0.3 fusion.18
  82.6 0.3 fusion.29
  83.2 0.6 fusion.110
  83.8 0.5 fusion.6
  84.3 0.5 fusion.5
  84.8 0.5 fusion.28
  85.3 0.5 multiply_reduce_fusion
  85.9 0.5 multiply_convert_fusion
  86.3 0.4 fusion.30
  86.8 0.5 fusion.27
  88.0 1.0 fusion.7
  89.0 1.2 fusion.4
  90.2 0.4 reshape.69
  90.7 48.0 %all_to_all.10 = bf16[256,6,4,128]{3,2,1,0:T(4,128)(2,1)S(1)} all-to-all(bf16[256,6,4,128]{3,2,1,0:T(4,128)(2,1)S(1)} %reshape.69), channel_id=1, replica_groups=mesh['seq'=64,'head'=4] {'head','seq'}, dimensions={0} | all-to-all | bytes 3145728 | tf_op jit(solution)/shard_map/all_to_all | solution.py:248
  138.7 3.3 %fusion.105 = (bf16[1,384,1,128]{3,2,1,0:T(2,128)(2,1)S(1)}, bf16[1,384,1,128]{3,2,1,0:T(2,128)(2,1)S(1)}, bf16[1,384,1,128]{3,2,1,0:T(2,128)(2,1)S(1)}, bf16[1,...) fusion(bf16[4,384,4,128]{3,2,1,0:T(4,128)(2,1)S(1)} %bitcast.206), kind=kLoop, calls=%fused_computation.181 | loop fusion | bytes 3145728 | tf_op jit(solution)/shard_map/slice | solution.py:255
  142.3 0.3 fusion.47
  142.6 0.3 fusion.46
  142.9 0.3 fusion.45
  143.3 0.9 copy.104
  144.5 0.3 fusion.42
  144.8 0.3 fusion.41
  145.2 0.3 fusion.40
  145.5 0.9 copy.103
  147.7 0.9 copy.102
  149.0 0.3 fusion.34
  149.3 0.3 fusion.33
  149.6 0.3 fusion.32
  150.0 0.9 copy.101
  (50 shorter events, 5.2 us)
Async XLA Ops:
  0.6 5.2 %copy-start.1 = (bf16[256,4,128]{2,1,0:T(4,128)(2,1)S(1)}, bf16[256,4,128]{2,1,0:T(4,128)(2,1)}, u32[]{:S(2)}) copy-start(bf16[256,4,128]{2,1,0:T(4,128)(2,1)} %param.7) | copy-start | bytes 786436
  0.6 5.2 %copy-start.2 = (bf16[256,4,128]{2,1,0:T(4,128)(2,1)S(1)}, bf16[256,4,128]{2,1,0:T(4,128)(2,1)}, u32[]{:S(2)}) copy-start(bf16[256,4,128]{2,1,0:T(4,128)(2,1)} %param.6) | copy-start | bytes 786436
  0.7 5.3 %copy-start.3 = (bf16[256,4,128]{2,1,0:T(4,128)(2,1)S(1)}, bf16[256,4,128]{2,1,0:T(4,128)(2,1)}, u32[]{:S(2)}) copy-start(bf16[256,4,128]{2,1,0:T(4,128)(2,1)} %param.9) | copy-start | bytes 786436
  0.7 5.3 %copy-start.4 = (bf16[256,4,128]{2,1,0:T(4,128)(2,1)S(1)}, bf16[256,4,128]{2,1,0:T(4,128)(2,1)}, u32[]{:S(2)}) copy-start(bf16[256,4,128]{2,1,0:T(4,128)(2,1)} %param.8) | copy-start | bytes 786436
  11.3 62.1 %all-to-all-start = ((bf16[256,13,2,128]{3,2,1,0:T(2,128)(2,1)}), bf16[256,13,2,128]{3,2,1,0:T(2,128)(2,1)S(1)}, u32[]{:S(2)}, u32[]{:S(2)}) async-start(bf16[256,13,2,128]{3,2,1,0:T(2,128)(2,1)} %pad_maximum_fusion), calls=%async_computation | async-start | bytes 3407872 | tf_op jit(solution)/shard_map/all_to_all | solution.py:214
  138.7 3.3 %copy-start = (pred[4,384,256]{2,1,0:T(32,128)(4,1)S(1)}, pred[4,384,256]{2,1,0:T(32,128)(4,1)}, u32[]{:S(2)}) copy-start(pred[4,384,256]{2,1,0:T(32,128)(4,1)} %get-tuple-element.49) | copy-start | bytes 1179652

commit v3 on v2

--- a/solution.py
+++ b/solution.py
@@ -246,18 +246,16 @@
         devices, capacity, 4, head_width
     )
     returned = lax.all_to_all(all_slots, order, 0, 0, tiled=True).reshape(
-        head_count, slot_count, 4, head_width
-    )
+        devices * capacity, 4, head_width
+    )
+    back_target = (jnp.arange(head_count, dtype=jnp.int32)[None, :] * slot_count + local_slot).reshape(-1)
+    back_hits = (
+        jnp.arange(devices * capacity, dtype=jnp.int32)[None, :] == back_target[:, None]
+    ).astype(jnp.bfloat16)
     return tuple(
-        jnp.stack(
-            [
-                jnp.dot(
-                    hits_low[head].T, returned[head, :, member], preferred_element_type=jnp.float32
-                ).astype(jnp.bfloat16)
-                for head in range(head_count)
-            ],
-            axis=1,
-        )
+        jnp.dot(back_hits, returned[:, member], preferred_element_type=jnp.float32)
+        .astype(jnp.bfloat16)
+        .reshape(sub_rows, head_count, head_width)
         for member in range(4)
     )
 

time: 151 us -> 151 us (level)
  blocking collectives: 48 us -> 0 us
  waiting for transfers between devices: 46.5 us -> 89 us
  starting transfers between devices: 15.6 us -> 21 us
  matrix products: 15.8 us -> 18.5 us
  local copies, waits for them, and re-layouts: 14.8 us -> 12.9 us
    all_to_all x1 -> x0, blocking collectives: 48 us -> none  [shards(): lax.all_to_all(all_slots, order, 0, 0, tiled=True)]
    all_to_all x0 -> x1, waiting for transfers between devices: none -> 42.5 us  [shards(): lax.all_to_all(all_slots, order, 0, 0, tiled=True)]
    all_to_all x0 -> x1, starting transfers between devices: none -> 5.4 us  [shards(): lax.all_to_all(all_slots, order, 0, 0, tiled=True)]
    unnamed x14 -> x4, local copies, waits for them, and re-layouts: 3.65 us -> 0.01 us
    dot_general x16 -> x4, matrix products: 5 us -> 7.65 us  [shards(): jnp.dot(back_hits, returned[:, member], preferred_element_type=jnp.float32)]
  transfers between devices with their start and end apart: 1 -> 2, of which waited for: 1 -> 2; matrix products, arithmetic and copies ran while one was open for 0% -> 0% of each run, Pallas kernels for 0% -> 0%
where the time goes in v3:
time: 151 us
  waiting for transfers between devices  89 us (59%)
  starting transfers between devices  21 us (14%)
  matrix products  18.5 us (12%)
  local copies, waits for them, and re-layouts  12.9 us (9%)
  other arithmetic  8.16 us (5%)
    all_to_all x1, waiting for transfers between devices, shards(): lax.all_to_all(payload, order, 0, 0, tiled=True)  46.5 us
    all_to_all x1, waiting for transfers between devices, shards(): lax.all_to_all(all_slots, order, 0, 0, tiled=True)  42.5 us
    all_to_all x1, starting transfers between devices, shards(): lax.all_to_all(payload, order, 0, 0, tiled=True)  15.6 us
    dot_general x4, matrix products, shards(): jnp.dot(back_hits, returned[:, member], preferred_element_type=jnp.float32)  7.65 us
    all_to_all x1, starting transfers between devices, shards(): lax.all_to_all(all_slots, order, 0, 0, tiled=True)  5.4 us
    concatenate x1, other arithmetic, shards(): jnp.concatenate((packed.reshape(devices, capacity * 2, 2, head_width), co...  3.42 us
  transfers between devices with their start and end apart: 2, of which 2 were waited for; matrix products, arithmetic and copies ran while one was open for 0% of the time, Pallas kernels for 0%

profile of v3, /device:TPU:1, one launch (start us, length us, event | category | flops | bytes accessed | tf_op | source)
XLA Modules:
  0.0 150.5 jit_solution(15702023710393267869)
XLA Ops:
  0.8 0.8 bitcast_compare_fusion
  1.6 0.9 fusion.44
  2.5 0.8 fusion.76
  3.3 0.3 fusion.21
  3.6 1.0 select_reduce_fusion
  4.6 0.1 select_n.41
  5.2 1.1 copy_bitcast_fusion.4
  6.4 0.6 convolution_convert_fusion
  7.0 1.2 copy.72
  8.2 3.4 %pad_maximum_fusion = bf16[256,13,2,128]{3,2,1,0:T(2,128)(2,1)} fusion(bf16[256,1,2,128]{3,2,1,0:T(2,128)(2,1)S(1)} %copy.99, bf16[256,12,2,128]{3,2,1,0:T(2,128)(2,1)S(1)} %bitcast.121), kind=kLoop, calls=%fused_computation.23 | loop fusion | flops 851968 | bytes 3407872 | tf_op jit(solution)/shard_map/concatenate | solution.py:210
  11.6 15.6 %all-to-all-start = ((bf16[256,13,2,128]{3,2,1,0:T(2,128)(2,1)}), bf16[256,13,2,128]{3,2,1,0:T(2,128)(2,1)S(1)}, u32[]{:S(2)}, u32[]{:S(2)}) async-start(bf16[256,13,2,128]{3,2,1,0:T(2,128)(2,1)} %pad_maximum_fusion), calls=%async_computation | async-start | bytes 3407872 | tf_op jit(solution)/shard_map/all_to_all | solution.py:214
  27.3 46.5 %all-to-all-done = bf16[256,13,2,128]{3,2,1,0:T(2,128)(2,1)S(1)} async-done(((bf16[256,13,2,128]{3,2,1,0:T(2,128)(2,1)}), bf16[256,13,2,128]{3,2,1,0:T(2,128)(2,1)S(1)}, u32[]{:S(2)}, u32[]{:S(2)}) %all-to-all-start) | async-done | bytes 1703968 | tf_op jit(solution)/shard_map/all_to_all | solution.py:214
  73.7 0.4 copy.76
  74.2 1.0 copy.77
  75.2 1.0 reshape.85
  76.5 1.0 fusion.29
  77.5 1.0 fusion.30
  78.6 0.5 reshape.86
  79.1 0.9 fusion.82
  80.0 1.1 fusion.81
  81.1 0.3 fusion.83
  81.4 0.2 fusion.53
  81.6 0.2 fusion.65
  81.8 0.3 fusion.78
  82.1 0.4 multiply_reduce_fusion.1
  82.6 0.3 fusion.28
  82.9 0.3 fusion.42
  83.2 0.3 fusion.75
  83.6 0.6 fusion.84
  84.1 0.5 fusion.14
  84.7 0.5 fusion.13
  85.1 0.5 fusion.41
  85.6 0.5 multiply_reduce_fusion
  86.2 0.5 multiply_convert_fusion
  86.6 0.4 fusion.43
  87.1 0.5 fusion.40
  87.8 0.2 copy.92
  88.1 0.2 copy.91
  88.3 1.0 fusion.15
  89.3 1.2 fusion.12
  90.6 1.9 %reshape.87 = bf16[256,6,4,128]{3,2,1,0:T(4,128)(2,1)} reshape(bf16[1536,512]{1,0:T(8,128)(2,1)S(1)} %fusion.12) | data formatting | bytes 3145728 | tf_op jit(solution)/shard_map/reshape | solution.py:245
  92.4 5.4 %all-to-all-start.1 = ((bf16[256,6,4,128]{3,2,1,0:T(4,128)(2,1)}), bf16[256,6,4,128]{3,2,1,0:T(4,128)(2,1)S(1)}, u32[]{:S(2)}, u32[]{:S(2)}) async-start(bf16[256,6,4,128]{3,2,1,0:T(4,128)(2,1)} %reshape.87), calls=%async_computation.1 | async-start | bytes 3145728 | tf_op jit(solution)/shard_map/all_to_all | solution.py:248
  98.1 42.5 %all-to-all-done.1 = bf16[256,6,4,128]{3,2,1,0:T(4,128)(2,1)S(1)} async-done(((bf16[256,6,4,128]{3,2,1,0:T(4,128)(2,1)}), bf16[256,6,4,128]{3,2,1,0:T(4,128)(2,1)S(1)}, u32[]{:S(2)}, u32[]{:S(2)}) %all-to-all-start.1) | async-done | bytes 1572896 | tf_op jit(solution)/shard_map/all_to_all | solution.py:248
  140.6 2.3 %fusion.79 = (bf16[1536,1,128]{2,1,0:T(2,128)(2,1)S(1)}, bf16[1536,1,128]{2,1,0:T(2,128)(2,1)S(1)}, bf16[1536,1,128]{2,1,0:T(2,128)(2,1)S(1)}, bf16[1536,1,128]{2,1,0:T(2,128)(2,1)S(1)}) fusion(bf16[1536,4,128]{2,1,0:T(4,128)(2,1)S(1)} %bitcast.118), kind=kLoop, calls=%fused_computation.133 | loop fusion | bytes 3145728 | tf_op jit(solution)/shard_map/slice | solution.py:256
  142.9 1.9 %fusion.39 = bf16[1024,128]{1,0:T(8,128)(2,1)} fusion(s32[1024]{0:T(1024)S(1)} %eq.89, bf16[1536,1,128]{2,1,0:T(2,128)(2,1)S(1)} %get-tuple-element.4), kind=kOutput, calls=%fused_computation.51 | convolution fusion | flops 404357120 | bytes 659456 | tf_op jit(solution)/shard_map/dot_general | solution.py:256
  144.8 1.9 %fusion.38 = bf16[1024,128]{1,0:T(8,128)(2,1)} fusion(s32[1024]{0:T(1024)S(1)} %eq.89, bf16[1536,1,128]{2,1,0:T(2,128)(2,1)S(1)} %get-tuple-element.5), kind=kOutput, calls=%fused_computation.50 | convolution fusion | flops 404357120 | bytes 659456 | tf_op jit(solution)/shard_map/dot_general | solution.py:256
  146.7 1.9 %fusion.37 = bf16[1024,128]{1,0:T(8,128)(2,1)} fusion(s32[1024]{0:T(1024)S(1)} %eq.89, bf16[1536,1,128]{2,1,0:T(2,128)(2,1)S(1)} %get-tuple-element.6), kind=kOutput, calls=%fused_computation.49 | convolution fusion | flops 404357120 | bytes 659456 | tf_op jit(solution)/shard_map/dot_general | solution.py:256
  148.6 1.9 %fusion.36 = bf16[1024,128]{1,0:T(8,128)(2,1)} fusion(s32[1024]{0:T(1024)S(1)} %eq.89, bf16[1536,1,128]{2,1,0:T(2,128)(2,1)S(1)} %get-tuple-element.7), kind=kOutput, calls=%fused_computation.48 | convolution fusion | flops 404357120 | bytes 659456 | tf_op jit(solution)/shard_map/dot_general | solution.py:256
  (28 shorter events, 1.5 us)
Async XLA Ops:
  0.6 5.7 %copy-start = (bf16[256,4,128]{2,1,0:T(4,128)(2,1)S(1)}, bf16[256,4,128]{2,1,0:T(4,128)(2,1)}, u32[]{:S(2)}) copy-start(bf16[256,4,128]{2,1,0:T(4,128)(2,1)} %param.9) | copy-start | bytes 786436
  0.6 5.7 %copy-start.1 = (bf16[256,4,128]{2,1,0:T(4,128)(2,1)S(1)}, bf16[256,4,128]{2,1,0:T(4,128)(2,1)}, u32[]{:S(2)}) copy-start(bf16[256,4,128]{2,1,0:T(4,128)(2,1)} %param.8) | copy-start | bytes 786436
  11.6 62.1 %all-to-all-start = ((bf16[256,13,2,128]{3,2,1,0:T(2,128)(2,1)}), bf16[256,13,2,128]{3,2,1,0:T(2,128)(2,1)S(1)}, u32[]{:S(2)}, u32[]{:S(2)}) async-start(bf16[256,13,2,128]{3,2,1,0:T(2,128)(2,1)} %pad_maximum_fusion), calls=%async_computation | async-start | bytes 3407872 | tf_op jit(solution)/shard_map/all_to_all | solution.py:214
  92.4 48.2 %all-to-all-start.1 = ((bf16[256,6,4,128]{3,2,1,0:T(4,128)(2,1)}), bf16[256,6,4,128]{3,2,1,0:T(4,128)(2,1)S(1)}, u32[]{:S(2)}, u32[]{:S(2)}) async-start(bf16[256,6,4,128]{3,2,1,0:T(4,128)(2,1)} %reshape.87), calls=%async_computation.1 | async-start | bytes 3145728 | tf_op jit(solution)/shard_map/all_to_all | solution.py:248

commit v4 on v3

--- a/solution.py
+++ b/solution.py
@@ -246,18 +246,12 @@
         devices, capacity, 4, head_width
     )
     returned = lax.all_to_all(all_slots, order, 0, 0, tiled=True).reshape(
-        devices * capacity, 4, head_width
-    )
-    back_target = (jnp.arange(head_count, dtype=jnp.int32)[None, :] * slot_count + local_slot).reshape(-1)
-    back_hits = (
-        jnp.arange(devices * capacity, dtype=jnp.int32)[None, :] == back_target[:, None]
-    ).astype(jnp.bfloat16)
-    return tuple(
-        jnp.dot(back_hits, returned[:, member], preferred_element_type=jnp.float32)
-        .astype(jnp.bfloat16)
-        .reshape(sub_rows, head_count, head_width)
-        for member in range(4)
-    )
+        head_count, slot_count, 4 * head_width
+    )
+    everything = jnp.einsum(
+        "hsr,hsf->rhf", hits_low, returned, preferred_element_type=jnp.float32
+    ).astype(jnp.bfloat16).reshape(sub_rows, head_count, 4, head_width)
+    return (everything[:, :, 0], everything[:, :, 1], everything[:, :, 2], everything[:, :, 3])
 
 
 def solution(mesh):

time: 151 us -> 144 us (0.954)
  blocking collectives: 0 us -> 48 us
  waiting for transfers between devices: 89 us -> 46.5 us
  matrix products: 18.5 us -> 11.6 us
  starting transfers between devices: 21 us -> 15.6 us
    all_to_all x0 -> x1, blocking collectives: none -> 48 us  [shards(): lax.all_to_all(all_slots, order, 0, 0, tiled=True)]
    all_to_all x1 -> x0, waiting for transfers between devices: 42.5 us -> none  [shards(): lax.all_to_all(all_slots, order, 0, 0, tiled=True)]
    dot_general x4 -> x1, matrix products: 7.65 us -> 0.84 us  [shards(): jnp.einsum('hsr,hsf->rhf', hits_low, returned, preferred_element_type=jnp...]
    all_to_all x1 -> x0, starting transfers between devices: 5.4 us -> none  [shards(): lax.all_to_all(all_slots, order, 0, 0, tiled=True)]
    unnamed x4 -> x8, local copies, waits for them, and re-layouts: 0.01 us -> 3.48 us
    slice x1, local copies, waits for them, and re-layouts: 2.28 us -> 0.07 us  [shards(): everything[:, :, 3]]
  transfers between devices with their start and end apart: 2 -> 1, of which waited for: 2 -> 1; matrix products, arithmetic and copies ran while one was open for 0% -> 0% of each run, Pallas kernels for 0% -> 0%
where the time goes in v4:
time: 144 us
  blocking collectives  48 us (33%)
  waiting for transfers between devices  46.5 us (32%)
  starting transfers between devices  15.6 us (11%)
  local copies, waits for them, and re-layouts  13.1 us (9%)
  matrix products  11.6 us (8%)
  other arithmetic  8.1 us (6%)
    all_to_all x1, blocking collectives, shards(): lax.all_to_all(all_slots, order, 0, 0, tiled=True)  48 us
    all_to_all x1, waiting for transfers between devices, shards(): lax.all_to_all(payload, order, 0, 0, tiled=True)  46.5 us
    all_to_all x1, starting transfers between devices, shards(): lax.all_to_all(payload, order, 0, 0, tiled=True)  15.6 us
    unnamed x8, local copies, waits for them, and re-layouts  3.48 us
    concatenate x1, other arithmetic, shards(): jnp.concatenate((packed.reshape(devices, capacity * 2, 2, head_width), co...  3.42 us
  transfers between devices with their start and end apart: 1, of which 1 were waited for; matrix products, arithmetic and copies ran while one was open for 0% of the time, Pallas kernels for 0%

profile of v4, /device:TPU:1, one launch (start us, length us, event | category | flops | bytes accessed | tf_op | source)
XLA Modules:
  0.0 144.0 jit_solution(4116794802866873800)
XLA Ops:
  0.7 0.8 bitcast_compare_fusion
  1.6 0.9 fusion.34
  2.5 0.7 add_bitcast_fusion
  3.2 0.3 fusion.14
  3.5 1.0 select_reduce_fusion
  4.5 0.1 select_n.41
  5.1 1.1 copy_bitcast_fusion.4
  6.3 0.6 convolution_convert_fusion
  6.9 1.2 copy.82
  8.1 3.4 %pad_maximum_fusion = bf16[256,13,2,128]{3,2,1,0:T(2,128)(2,1)} fusion(bf16[256,1,2,128]{3,2,1,0:T(2,128)(2,1)S(1)} %copy.115, bf16[256,12,2,128]{3,2,1,0:T(2,128)(2,1)S(1)} %bitcast.111), kind=kLoop, calls=%fused_computation.14 | loop fusion | flops 851968 | bytes 3407872 | tf_op jit(solution)/shard_map/concatenate | solution.py:210
  11.6 15.6 %all-to-all-start = ((bf16[256,13,2,128]{3,2,1,0:T(2,128)(2,1)}), bf16[256,13,2,128]{3,2,1,0:T(2,128)(2,1)S(1)}, u32[]{:S(2)}, u32[]{:S(2)}) async-start(bf16[256,13,2,128]{3,2,1,0:T(2,128)(2,1)} %pad_maximum_fusion), calls=%async_computation | async-start | bytes 3407872 | tf_op jit(solution)/shard_map/all_to_all | solution.py:214
  27.2 46.5 %all-to-all-done = bf16[256,13,2,128]{3,2,1,0:T(2,128)(2,1)S(1)} async-done(((bf16[256,13,2,128]{3,2,1,0:T(2,128)(2,1)}), bf16[256,13,2,128]{3,2,1,0:T(2,128)(2,1)S(1)}, u32[]{:S(2)}, u32[]{:S(2)}) %all-to-all-start) | async-done | bytes 1703968 | tf_op jit(solution)/shard_map/all_to_all | solution.py:214
  73.7 0.4 copy.86
  74.2 1.0 copy.87
  75.2 1.0 reshape.70
  76.4 1.0 fusion.23
  77.4 1.0 fusion.24
  78.5 0.5 reshape.71
  79.0 0.9 fusion.64
  80.0 1.1 fusion.63
  81.0 0.3 fusion.65
  81.4 0.2 fusion.43
  81.6 0.2 fusion.48
  81.7 0.3 fusion.60
  82.1 0.4 multiply_reduce_fusion.1
  82.5 0.3 fusion.22
  82.8 0.3 fusion.32
  83.2 0.3 fusion.58
  83.5 0.6 fusion.66
  84.1 0.5 fusion.6
  84.6 0.5 fusion.5
  85.1 0.5 fusion.31
  85.6 0.5 multiply_reduce_fusion
  86.1 0.5 multiply_convert_fusion
  86.6 0.4 fusion.33
  87.0 0.5 fusion.30
  87.8 0.2 copy.102
  88.0 0.2 copy.101
  88.2 1.0 fusion.7
  89.3 1.2 fusion.4
  90.5 0.4 reshape.72
  90.9 48.0 %all_to_all.10 = bf16[256,6,4,128]{3,2,1,0:T(4,128)(2,1)S(1)} all-to-all(bf16[256,6,4,128]{3,2,1,0:T(4,128)(2,1)S(1)} %reshape.72), channel_id=1, replica_groups=mesh['seq'=64,'head'=4] {'head','seq'}, dimensions={0} | all-to-all | bytes 3145728 | tf_op jit(solution)/shard_map/all_to_all | solution.py:248
  138.9 0.6 reshape.73
  139.6 0.8 fusion.19
  140.5 0.9 copy.127
  141.3 0.9 copy.126
  142.2 0.9 copy.125
  143.1 0.9 copy.124
  (26 shorter events, 1.3 us)
Async XLA Ops:
  0.6 5.6 %copy-start = (bf16[256,4,128]{2,1,0:T(4,128)(2,1)S(1)}, bf16[256,4,128]{2,1,0:T(4,128)(2,1)}, u32[]{:S(2)}) copy-start(bf16[256,4,128]{2,1,0:T(4,128)(2,1)} %param.9) | copy-start | bytes 786436
  0.6 5.6 %copy-start.1 = (bf16[256,4,128]{2,1,0:T(4,128)(2,1)S(1)}, bf16[256,4,128]{2,1,0:T(4,128)(2,1)}, u32[]{:S(2)}) copy-start(bf16[256,4,128]{2,1,0:T(4,128)(2,1)} %param.8) | copy-start | bytes 786436
  11.6 62.1 %all-to-all-start = ((bf16[256,13,2,128]{3,2,1,0:T(2,128)(2,1)}), bf16[256,13,2,128]{3,2,1,0:T(2,128)(2,1)S(1)}, u32[]{:S(2)}, u32[]{:S(2)}) async-start(bf16[256,13,2,128]{3,2,1,0:T(2,128)(2,1)} %pad_maximum_fusion), calls=%async_computation | async-start | bytes 3407872 | tf_op jit(solution)/shard_map/all_to_all | solution.py:214

commit v5 on v4

--- a/solution.py
+++ b/solution.py
@@ -1,8 +1,11 @@
+import functools
 import math
 
 import jax
 import jax.numpy as jnp
 from jax import lax
+from jax.experimental import pallas as pl
+from jax.experimental.pallas import tpu as pltpu
 from jax.sharding import PartitionSpec as P
 
 
@@ -180,6 +183,60 @@
     grad_key_block = (grad_key_sum * score_scale).astype(jnp.bfloat16)
     grad_value_block = grad_value_sum.astype(jnp.bfloat16)
     return jnp.stack((grad_query_block, grad_key_block, grad_value_block), axis=1)
+
+
+def attention_kernel(x_ref, out_ref, dk_acc, dv_acc, *, block_rows, head_width):
+    rows = x_ref.shape[0]
+    scale = 1.0 / math.sqrt(head_width)
+    dk_acc[...] = jnp.zeros_like(dk_acc)
+    dv_acc[...] = jnp.zeros_like(dv_acc)
+    for block_index in range(rows // block_rows):
+        start = block_index * block_rows
+        finish = start + block_rows
+        q_part = x_ref[start:finish, 0:head_width]
+        g_part = x_ref[start:finish, 3 * head_width : 4 * head_width]
+        k_seen = x_ref[0:finish, head_width : 2 * head_width]
+        v_seen = x_ref[0:finish, 2 * head_width : 3 * head_width]
+        scores = (
+            lax.dot_general(q_part, k_seen, (((1,), (1,)), ((), ())), preferred_element_type=jnp.float32)
+            * scale
+        )
+        row_ids = start + lax.broadcasted_iota(jnp.int32, scores.shape, 0)
+        col_ids = lax.broadcasted_iota(jnp.int32, scores.shape, 1)
+        scores = jnp.where(col_ids <= row_ids, scores, -jnp.inf)
+        row_top = jnp.max(scores, axis=1, keepdims=True)
+        weights = jnp.exp(scores - row_top)
+        probabilities = weights / jnp.sum(weights, axis=1, keepdims=True)
+        probs_low = probabilities.astype(jnp.bfloat16)
+        attended = jnp.dot(probs_low, v_seen, preferred_element_type=jnp.float32).astype(jnp.bfloat16)
+        out_ref[start:finish, 0:head_width] = attended
+        grad_prob = lax.dot_general(
+            g_part, v_seen, (((1,), (1,)), ((), ())), preferred_element_type=jnp.float32
+        )
+        row_delta = jnp.sum(
+            g_part.astype(jnp.float32) * attended.astype(jnp.float32), axis=1, keepdims=True
+        )
+        grad_score = (probabilities * (grad_prob - row_delta)).astype(jnp.bfloat16)
+        out_ref[start:finish, head_width : 2 * head_width] = (
+            jnp.dot(grad_score, k_seen, preferred_element_type=jnp.float32) * scale
+        ).astype(jnp.bfloat16)
+        dk_acc[0:finish, :] += lax.dot_general(
+            grad_score, q_part, (((0,), (0,)), ((), ())), preferred_element_type=jnp.float32
+        )
+        dv_acc[0:finish, :] += lax.dot_general(
+            probs_low, g_part, (((0,), (0,)), ((), ())), preferred_element_type=jnp.float32
+        )
+    out_ref[:, 2 * head_width : 3 * head_width] = (dk_acc[...] * scale).astype(jnp.bfloat16)
+    out_ref[:, 3 * head_width : 4 * head_width] = dv_acc[...].astype(jnp.bfloat16)
+
+
+def fused_attention(ordered_flat, head_width, block_rows=256):
+    rows, width = ordered_flat.shape
+    return pl.pallas_call(
+        functools.partial(attention_kernel, block_rows=block_rows, head_width=head_width),
+        out_shape=jax.ShapeDtypeStruct((rows, width), jnp.bfloat16),
+        scratch_shapes=[pltpu.VMEM((rows, head_width), jnp.float32)] * 2,
+    )(ordered_flat)
 
 
 def shards(query_rows, key_rows, value_rows, grad_rows, assignment, position):
@@ -219,29 +276,7 @@
     ).astype(jnp.int32).reshape(-1)
     block_rows = min(512, cluster_len)
     tables = place_tables(flat_place, cluster_len, block_rows)
-    ordered = slots_to_order(tables, arrived_data).reshape(cluster_len, 4, head_width)
-    query_block = ordered[:, 0]
-    key_block = ordered[:, 1]
-    value_block = ordered[:, 2]
-    grad_block = ordered[:, 3]
-    score_scale = 1.0 / math.sqrt(head_width)
-    attended_block, row_tops, row_totals = forward_pass(
-        query_block, key_block, value_block, block_rows, score_scale
-    )
-    grads_block = backward_pass(
-        query_block,
-        key_block,
-        value_block,
-        grad_block,
-        attended_block,
-        row_tops,
-        row_totals,
-        block_rows,
-        score_scale,
-    )
-    combined = jnp.concatenate((attended_block[:, None], grads_block), axis=1).reshape(
-        cluster_len, 4 * head_width
-    )
+    combined = fused_attention(slots_to_order(tables, arrived_data), head_width)
     all_slots = order_to_slots(tables, combined, block_rows).reshape(
         devices, capacity, 4, head_width
     )

time: 144 us -> 142 us (0.986)
  Pallas kernels: 0 us -> 6.24 us
  local copies, waits for them, and re-layouts: 13.1 us -> 9.08 us
  matrix products: 11.6 us -> 7.66 us
    pallas_call x0 -> x1, Pallas kernels: none -> 6.24 us  [fused_attention(): pl.pallas_call(functools.partial(attention_kernel, block_rows=block_rows,...]
    dot_general x12 -> x0, matrix products: 5.01 us -> none  [the longest x2 0.96 us: forward_pass(): jnp.dot(probs_low, value_block[:finish], preferred_element_type=jnp.float32)]
    slice x5 -> x0, local copies, waits for them, and re-layouts: 2.53 us -> none  [the longest x1 1.08 us: forward_pass(): value_block[:finish]]
    unnamed x8 -> x14, local copies, waits for them, and re-layouts: 3.48 us -> 3.49 us
where the time goes in v5:
time: 142 us
  blocking collectives  48 us (34%)
  waiting for transfers between devices  46.4 us (33%)
  starting transfers between devices  15.7 us (11%)
  local copies, waits for them, and re-layouts  9.08 us (6%)
  matrix products  7.66 us (5%)
  other arithmetic  7.55 us (5%)
  Pallas kernels  6.24 us (4%)
    all_to_all x1, blocking collectives, shards(): lax.all_to_all(all_slots, order, 0, 0, tiled=True)  48 us
    all_to_all x1, waiting for transfers between devices, shards(): lax.all_to_all(payload, order, 0, 0, tiled=True)  46.4 us
    all_to_all x1, starting transfers between devices, shards(): lax.all_to_all(payload, order, 0, 0, tiled=True)  15.7 us
    pallas_call x1, Pallas kernels, fused_attention(): pl.pallas_call(functools.partial(attention_kernel, block_rows=block_rows,...  6.24 us
    unnamed x14, local copies, waits for them, and re-layouts  3.49 us
    concatenate x1, other arithmetic, shards(): jnp.concatenate((packed.reshape(devices, capacity * 2, 2, head_width), co...  3.42 us
    dot_general x2, matrix products, order_to_slots(): jnp.einsum('la,lf->af', table, piece, preferred_element_type=jnp.float32)  3.31 us
  transfers between devices with their start and end apart: 1, of which 1 were waited for; matrix products, arithmetic and copies ran while one was open for 0% of the time, Pallas kernels for 0%

profile of v5, /device:TPU:1, one launch (start us, length us, event | category | flops | bytes accessed | tf_op | source)
XLA Modules:
  0.0 141.6 jit_solution(16707314579110506382)
XLA Ops:
  0.6 0.0 copy-start.1
  0.6 0.0 copy-start.2
  0.7 0.0 copy-start.3
  0.7 0.0 copy-start.4
  0.7 0.1 eq.72
  0.8 0.9 bitcast_compare_fusion
  1.6 0.9 fusion.27
  2.6 0.7 add_bitcast_fusion
  3.3 0.3 fusion.17
  3.6 1.0 select_reduce_fusion
  4.5 0.1 select_n.31
  4.7 0.1 add_select_fusion.1
  4.8 0.1 copy.46
  4.9 0.1 copy.47
  5.0 0.1 copy.58
  5.1 0.0 copy-done.1
  5.2 0.0 copy-done.2
  5.2 0.1 copy_bitcast_fusion.2
  5.2 0.0 copy-done.3
  5.3 0.0 copy-done.4
  5.3 0.1 copy_bitcast_fusion
  5.3 0.6 convolution_convert_fusion
  5.9 1.2 copy.45
  7.2 3.4 %pad_maximum_fusion = bf16[256,13,2,128]{3,2,1,0:T(2,128)(2,1)} fusion(bf16[256,1,2,128]{3,2,1,0:T(2,128)(2,1)S(1)} %copy.58, bf16[256,12,2,128]{3,2,1,0:T(2,128)(2,1)S(1)} %bitcast.45), kind=kLoop, calls=%fused_computation.9 | loop fusion | flops 851968 | bytes 3407872 | tf_op jit(solution)/shard_map/concatenate | solution.py:267
  10.6 15.7 %all-to-all-start = ((bf16[256,13,2,128]{3,2,1,0:T(2,128)(2,1)}), bf16[256,13,2,128]{3,2,1,0:T(2,128)(2,1)S(1)}, u32[]{:S(2)}, u32[]{:S(2)}) async-start(bf16[256,13,2,128]{3,2,1,0:T(2,128)(2,1)} %pad_maximum_fusion), calls=%async_computation | async-start | bytes 3407872 | tf_op jit(solution)/shard_map/all_to_all | solution.py:271
  26.3 46.4 %all-to-all-done = bf16[256,13,2,128]{3,2,1,0:T(2,128)(2,1)S(1)} async-done(((bf16[256,13,2,128]{3,2,1,0:T(2,128)(2,1)}), bf16[256,13,2,128]{3,2,1,0:T(2,128)(2,1)S(1)}, u32[]{:S(2)}, u32[]{:S(2)}) %all-to-all-start) | async-done | bytes 1703968 | tf_op jit(solution)/shard_map/all_to_all | solution.py:271
  72.7 0.4 copy.49
  73.1 0.1 slice.43
  73.2 1.0 copy.50
  74.2 1.0 reshape.52
  75.2 0.1 fusion.44
  75.3 0.1 eq.77
  75.5 1.0 fusion.23
  76.5 1.0 fusion.24
  77.5 1.0 pad_maximum_fusion.1.x_ref
  78.5 6.2 %shard_map.93 = bf16[1024,512]{1,0:T(8,128)(2,1)} custom-call(bf16[1024,512]{1,0:T(8,128)(2,1)} %pad_maximum_fusion.1.x_ref), custom_call_target="tpu_custom_call" | custom-call | tf_op jit(solution)/shard_map/pallas_call | solution.py:235
  84.8 2.2 %fusion.7 = f32[1536,512]{1,0:T(8,128)S(1)} fusion(s32[1536]{0:T(1024)S(1)} %eq.77, bf16[1024,512]{1,0:T(8,128)(2,1)} %shard_map.93), kind=kOutput, calls=%fused_computation.6 | convolution fusion | flops 806092800 | bytes 3676160 | tf_op jit(solution)/shard_map/la,lf->af/dot_general | solution.py:85
  86.9 0.0 copy-done
  86.9 1.1 fusion.9
  88.1 0.4 reshape.53
  88.5 48.0 %all_to_all.10 = bf16[256,6,4,128]{3,2,1,0:T(4,128)(2,1)S(1)} all-to-all(bf16[256,6,4,128]{3,2,1,0:T(4,128)(2,1)S(1)} %reshape.53), channel_id=1, replica_groups=mesh['seq'=64,'head'=4] {'head','seq'}, dimensions={0} | all-to-all | bytes 3145728 | tf_op jit(solution)/shard_map/all_to_all | solution.py:283
  136.5 0.6 reshape.54
  137.2 0.8 fusion.22
  138.0 0.1 fusion.49
  138.1 0.9 copy.62
  139.0 0.9 copy.61
  139.8 0.9 copy.60
  140.7 0.9 copy.59
  (8 shorter events, 0.1 us)
Async XLA Ops:
  0.6 4.5 %copy-start.1 = (bf16[256,4,128]{2,1,0:T(4,128)(2,1)S(1)}, bf16[256,4,128]{2,1,0:T(4,128)(2,1)}, u32[]{:S(2)}) copy-start(bf16[256,4,128]{2,1,0:T(4,128)(2,1)} %param.7) | copy-start | bytes 786436
  0.6 4.5 %copy-start.2 = (bf16[256,4,128]{2,1,0:T(4,128)(2,1)S(1)}, bf16[256,4,128]{2,1,0:T(4,128)(2,1)}, u32[]{:S(2)}) copy-start(bf16[256,4,128]{2,1,0:T(4,128)(2,1)} %param.6) | copy-start | bytes 786436
  0.7 4.6 %copy-start.3 = (bf16[256,4,128]{2,1,0:T(4,128)(2,1)S(1)}, bf16[256,4,128]{2,1,0:T(4,128)(2,1)}, u32[]{:S(2)}) copy-start(bf16[256,4,128]{2,1,0:T(4,128)(2,1)} %param.9) | copy-start | bytes 786436
  0.7 4.6 %copy-start.4 = (bf16[256,4,128]{2,1,0:T(4,128)(2,1)S(1)}, bf16[256,4,128]{2,1,0:T(4,128)(2,1)}, u32[]{:S(2)}) copy-start(bf16[256,4,128]{2,1,0:T(4,128)(2,1)} %param.8) | copy-start | bytes 786436
  10.6 62.1 %all-to-all-start = ((bf16[256,13,2,128]{3,2,1,0:T(2,128)(2,1)}), bf16[256,13,2,128]{3,2,1,0:T(2,128)(2,1)S(1)}, u32[]{:S(2)}, u32[]{:S(2)}) async-start(bf16[256,13,2,128]{3,2,1,0:T(2,128)(2,1)} %pad_maximum_fusion), calls=%async_computation | async-start | bytes 3407872 | tf_op jit(solution)/shard_map/all_to_all | solution.py:271
  84.8 2.2 %copy-start = (bf16[1024,512]{1,0:T(8,128)(2,1)S(1)}, bf16[1024,512]{1,0:T(8,128)(2,1)}, u32[]{:S(2)}) copy-start(bf16[1024,512]{1,0:T(8,128)(2,1)} %shard_map.93) | copy-start | bytes 3145732

commit v6 on v5

--- a/solution.py
+++ b/solution.py
@@ -185,9 +185,16 @@
     return jnp.stack((grad_query_block, grad_key_block, grad_value_block), axis=1)
 
 
-def attention_kernel(x_ref, out_ref, dk_acc, dv_acc, *, block_rows, head_width):
-    rows = x_ref.shape[0]
+def attention_kernel(place_ref, arrived_ref, out_ref, x_ref, y_ref, dk_acc, dv_acc, *, block_rows):
+    rows, width = x_ref.shape
+    head_width = width // 4
     scale = 1.0 / math.sqrt(head_width)
+    order = (
+        lax.broadcasted_iota(jnp.int32, (rows, place_ref.shape[1]), 0) == place_ref[...]
+    ).astype(jnp.bfloat16)
+    x_ref[...] = jnp.dot(order, arrived_ref[...], preferred_element_type=jnp.float32).astype(
+        jnp.bfloat16
+    )
     dk_acc[...] = jnp.zeros_like(dk_acc)
     dv_acc[...] = jnp.zeros_like(dv_acc)
     for block_index in range(rows // block_rows):
@@ -209,7 +216,7 @@
         probabilities = weights / jnp.sum(weights, axis=1, keepdims=True)
         probs_low = probabilities.astype(jnp.bfloat16)
         attended = jnp.dot(probs_low, v_seen, preferred_element_type=jnp.float32).astype(jnp.bfloat16)
-        out_ref[start:finish, 0:head_width] = attended
+        y_ref[start:finish, 0:head_width] = attended
         grad_prob = lax.dot_general(
             g_part, v_seen, (((1,), (1,)), ((), ())), preferred_element_type=jnp.float32
         )
@@ -217,7 +224,7 @@
             g_part.astype(jnp.float32) * attended.astype(jnp.float32), axis=1, keepdims=True
         )
         grad_score = (probabilities * (grad_prob - row_delta)).astype(jnp.bfloat16)
-        out_ref[start:finish, head_width : 2 * head_width] = (
+        y_ref[start:finish, head_width : 2 * head_width] = (
             jnp.dot(grad_score, k_seen, preferred_element_type=jnp.float32) * scale
         ).astype(jnp.bfloat16)
         dk_acc[0:finish, :] += lax.dot_general(
@@ -226,17 +233,25 @@
         dv_acc[0:finish, :] += lax.dot_general(
             probs_low, g_part, (((0,), (0,)), ((), ())), preferred_element_type=jnp.float32
         )
-    out_ref[:, 2 * head_width : 3 * head_width] = (dk_acc[...] * scale).astype(jnp.bfloat16)
-    out_ref[:, 3 * head_width : 4 * head_width] = dv_acc[...].astype(jnp.bfloat16)
-
-
-def fused_attention(ordered_flat, head_width, block_rows=256):
-    rows, width = ordered_flat.shape
+    y_ref[:, 2 * head_width : 3 * head_width] = (dk_acc[...] * scale).astype(jnp.bfloat16)
+    y_ref[:, 3 * head_width : 4 * head_width] = dv_acc[...].astype(jnp.bfloat16)
+    out_ref[...] = lax.dot_general(
+        order, y_ref[...], (((0,), (0,)), ((), ())), preferred_element_type=jnp.float32
+    ).astype(jnp.bfloat16)
+
+
+def fused_attention(flat_place, arrived_flat, cluster_len, block_rows=256):
+    slots, width = arrived_flat.shape
     return pl.pallas_call(
-        functools.partial(attention_kernel, block_rows=block_rows, head_width=head_width),
-        out_shape=jax.ShapeDtypeStruct((rows, width), jnp.bfloat16),
-        scratch_shapes=[pltpu.VMEM((rows, head_width), jnp.float32)] * 2,
-    )(ordered_flat)
+        functools.partial(attention_kernel, block_rows=block_rows),
+        out_shape=jax.ShapeDtypeStruct((slots, width), jnp.bfloat16),
+        scratch_shapes=[
+            pltpu.VMEM((cluster_len, width), jnp.bfloat16),
+            pltpu.VMEM((cluster_len, width), jnp.bfloat16),
+            pltpu.VMEM((cluster_len, width // 4), jnp.float32),
+            pltpu.VMEM((cluster_len, width // 4), jnp.float32),
+        ],
+    )(flat_place.reshape(1, slots), arrived_flat)
 
 
 def shards(query_rows, key_rows, value_rows, grad_rows, assignment, position):
@@ -274,10 +289,7 @@
     flat_place = (
         arrived_code[:, :capacity] * 32.0 + arrived_code[:, capacity : 2 * capacity]
     ).astype(jnp.int32).reshape(-1)
-    block_rows = min(512, cluster_len)
-    tables = place_tables(flat_place, cluster_len, block_rows)
-    combined = fused_attention(slots_to_order(tables, arrived_data), head_width)
-    all_slots = order_to_slots(tables, combined, block_rows).reshape(
+    all_slots = fused_attention(flat_place, arrived_data, cluster_len).reshape(
         devices, capacity, 4, head_width
     )
     returned = lax.all_to_all(all_slots, order, 0, 0, tiled=True).reshape(

time: 142 us -> 142 us (level)
  blocking collectives: 48 us -> 110 us
  waiting for transfers between devices: 46.4 us -> 0 us
  starting transfers between devices: 15.7 us -> 0 us
  matrix products: 7.66 us -> 2.35 us
  local copies, waits for them, and re-layouts: 9.08 us -> 12.9 us
  Pallas kernels: 6.24 us -> 9.9 us
  other arithmetic: 7.55 us -> 5.32 us
    all_to_all x0 -> x1, blocking collectives: none -> 61.9 us  [shards(): lax.all_to_all(payload, order, 0, 0, tiled=True)]
    all_to_all x1 -> x0, waiting for transfers between devices: 46.4 us -> none  [shards(): lax.all_to_all(payload, order, 0, 0, tiled=True)]
    all_to_all x1 -> x0, starting transfers between devices: 15.7 us -> none  [shards(): lax.all_to_all(payload, order, 0, 0, tiled=True)]
    dot_general x4 -> x0, matrix products: 5.31 us -> none  [the longest x2 3.31 us: order_to_slots(): jnp.einsum('la,lf->af', table, piece, preferred_element_type=jnp.float32)]
    pallas_call x1, Pallas kernels: 6.24 us -> 9.9 us  [fused_attention(): pl.pallas_call(functools.partial(attention_kernel, block_rows=block_rows)...]
    reshape x1, local copies, waits for them, and re-layouts: 0.42 us -> 2.36 us  [shards(): fused_attention(flat_place, arrived_data, cluster_len)]
    unnamed x14 -> x12, local copies, waits for them, and re-layouts: 3.49 us -> 3.49 us
  transfers between devices with their start and end apart: 1 -> 0, of which waited for: 1 -> 0; matrix products, arithmetic and copies ran while one was open for 0% -> 0% of each run, Pallas kernels for 0% -> 0%
where the time goes in v6:
time: 142 us; the launch traced here: 141 us
  blocking collectives  110 us (77%)
  local copies, waits for them, and re-layouts  12.9 us (9%)
  Pallas kernels  9.9 us (7%)
  other arithmetic  5.32 us (4%)
  matrix products  2.35 us (2%)
    all_to_all x1, blocking collectives, shards(): lax.all_to_all(payload, order, 0, 0, tiled=True)  61.9 us
    all_to_all x1, blocking collectives, shards(): lax.all_to_all(all_slots, order, 0, 0, tiled=True)  48 us
    pallas_call x1, Pallas kernels, fused_attention(): pl.pallas_call(functools.partial(attention_kernel, block_rows=block_rows)...  9.9 us
    unnamed x12, local copies, waits for them, and re-layouts  3.49 us

profile of v6, /device:TPU:1, one launch (start us, length us, event | category | flops | bytes accessed | tf_op | source)
XLA Modules:
  0.0 141.2 jit_solution(18253831010598704797)
XLA Ops:
  0.6 0.0 copy-start
  0.6 0.0 copy-start.1
  0.7 0.0 copy-start.2
  0.7 0.0 copy-start.3
  0.7 0.1 eq.45
  0.8 0.9 bitcast_compare_fusion
  1.6 0.9 fusion.5
  2.6 0.7 add_bitcast_fusion
  3.3 0.3 fusion.1
  3.6 1.0 select_reduce_fusion
  4.5 0.1 select_n.31
  4.7 0.1 add_select_fusion.1
  4.8 0.1 copy.35
  4.9 0.1 copy.36
  5.0 0.1 copy.47
  5.1 0.0 copy-done
  5.2 0.0 copy-done.1
  5.2 0.1 copy_bitcast_fusion.2
  5.2 0.0 copy-done.2
  5.3 0.0 copy-done.3
  5.3 0.1 copy_bitcast_fusion
  5.3 0.6 convolution_convert_fusion
  5.9 1.2 copy.34
  7.2 2.2 %pad_maximum_fusion = bf16[256,13,2,128]{3,2,1,0:T(2,128)(2,1)S(1)} fusion(bf16[256,1,2,128]{3,2,1,0:T(2,128)(2,1)S(1)} %copy.47, bf16[256,12,2,128]{3,2,1,0:T(2,128)(2,1)S(1)} %bitcast.43), kind=kLoop, calls=%fused_computation | loop fusion | flops 851968 | bytes 3407872 | tf_op jit(solution)/shard_map/concatenate | solution.py:282
  9.4 61.9 %all_to_all.10 = bf16[256,13,2,128]{3,2,1,0:T(2,128)(2,1)S(1)} all-to-all(bf16[256,13,2,128]{3,2,1,0:T(2,128)(2,1)S(1)} %pad_maximum_fusion), channel_id=1, replica_groups=mesh['seq'=64,'head'=4] {'head','seq'}, dimensions={0} | all-to-all | bytes 3407872 | tf_op jit(solution)/shard_map/all_to_all | solution.py:286
  71.3 0.4 copy.38
  71.7 0.1 slice.35
  71.8 1.0 copy.39
  72.8 2.3 %reshape.47.arrived_ref = bf16[1536,512]{1,0:T(8,128)(2,1)} reshape(bf16[256,24,128]{2,1,0:T(8,128)(2,1)S(1)} %copy.39) | data formatting | bytes 3145728 | tf_op jit(solution)/shard_map/reshape | solution.py:287
  75.1 0.1 fusion.20
  75.2 0.7 reshape_reshape.3.place_ref
  75.9 9.9 %shard_map.93 = bf16[1536,512]{1,0:T(8,128)(2,1)} custom-call(s32[1,1536]{1,0:T(1,128)} %reshape_reshape.3.place_ref, bf16[1536,512]{1,0:T(8,128)(2,1)} %reshape.47.arrived_ref), custom_call_target="tpu_custom_call" | custom-call | tf_op jit(solution)/shard_map/pallas_call | solution.py:245
  85.8 2.4 %reshape.48 = bf16[256,6,4,128]{3,2,1,0:T(4,128)(2,1)S(1)} reshape(bf16[1536,512]{1,0:T(8,128)(2,1)} %shard_map.93) | data formatting | bytes 3145728 | tf_op jit(solution)/shard_map/reshape | solution.py:292
  88.2 48.0 %all_to_all.11 = bf16[256,6,4,128]{3,2,1,0:T(4,128)(2,1)S(1)} all-to-all(bf16[256,6,4,128]{3,2,1,0:T(4,128)(2,1)S(1)} %reshape.48), channel_id=1, replica_groups=mesh['seq'=64,'head'=4] {'head','seq'}, dimensions={0} | all-to-all | bytes 3145728 | tf_op jit(solution)/shard_map/all_to_all | solution.py:295
  136.2 0.6 reshape.49
  136.8 0.8 fusion.4
  137.7 0.1 fusion.25
  137.7 0.9 copy.51
  138.6 0.9 copy.50
  139.5 0.9 copy.49
  140.4 0.9 copy.48
  (6 shorter events, 0.1 us)
Async XLA Ops:
  0.6 4.5 %copy-start = (bf16[256,4,128]{2,1,0:T(4,128)(2,1)S(1)}, bf16[256,4,128]{2,1,0:T(4,128)(2,1)}, u32[]{:S(2)}) copy-start(bf16[256,4,128]{2,1,0:T(4,128)(2,1)} %param.7) | copy-start | bytes 786436
  0.6 4.5 %copy-start.1 = (bf16[256,4,128]{2,1,0:T(4,128)(2,1)S(1)}, bf16[256,4,128]{2,1,0:T(4,128)(2,1)}, u32[]{:S(2)}) copy-start(bf16[256,4,128]{2,1,0:T(4,128)(2,1)} %param.6) | copy-start | bytes 786436
  0.7 4.6 %copy-start.2 = (bf16[256,4,128]{2,1,0:T(4,128)(2,1)S(1)}, bf16[256,4,128]{2,1,0:T(4,128)(2,1)}, u32[]{:S(2)}) copy-start(bf16[256,4,128]{2,1,0:T(4,128)(2,1)} %param.9) | copy-start | bytes 786436
  0.7 4.6 %copy-start.3 = (bf16[256,4,128]{2,1,0:T(4,128)(2,1)S(1)}, bf16[256,4,128]{2,1,0:T(4,128)(2,1)}, u32[]{:S(2)}) copy-start(bf16[256,4,128]{2,1,0:T(4,128)(2,1)} %param.8) | copy-start | bytes 786436

commit v7 on v6

--- a/solution.py
+++ b/solution.py
@@ -185,7 +185,7 @@
     return jnp.stack((grad_query_block, grad_key_block, grad_value_block), axis=1)
 
 
-def attention_kernel(place_ref, arrived_ref, out_ref, x_ref, y_ref, dk_acc, dv_acc, *, block_rows):
+def attention_kernel(place_ref, place_col_ref, arrived_ref, out_ref, x_ref, y_ref, dk_acc, dv_acc, *, block_rows):
     rows, width = x_ref.shape
     head_width = width // 4
     scale = 1.0 / math.sqrt(head_width)
@@ -235,12 +235,15 @@
         )
     y_ref[:, 2 * head_width : 3 * head_width] = (dk_acc[...] * scale).astype(jnp.bfloat16)
     y_ref[:, 3 * head_width : 4 * head_width] = dv_acc[...].astype(jnp.bfloat16)
-    out_ref[...] = lax.dot_general(
-        order, y_ref[...], (((0,), (0,)), ((), ())), preferred_element_type=jnp.float32
-    ).astype(jnp.bfloat16)
-
-
-def fused_attention(flat_place, arrived_flat, cluster_len, block_rows=256):
+    back = (
+        lax.broadcasted_iota(jnp.int32, (place_col_ref.shape[0], rows), 1) == place_col_ref[...]
+    ).astype(jnp.bfloat16)
+    out_ref[...] = jnp.dot(back, y_ref[...], preferred_element_type=jnp.float32).astype(
+        jnp.bfloat16
+    )
+
+
+def fused_attention(flat_place, arrived_flat, cluster_len, block_rows=128):
     slots, width = arrived_flat.shape
     return pl.pallas_call(
         functools.partial(attention_kernel, block_rows=block_rows),
@@ -251,7 +254,7 @@
             pltpu.VMEM((cluster_len, width // 4), jnp.float32),
             pltpu.VMEM((cluster_len, width // 4), jnp.float32),
         ],
-    )(flat_place.reshape(1, slots), arrived_flat)
+    )(flat_place.reshape(1, slots), flat_place.reshape(slots, 1), arrived_flat)
 
 
 def shards(query_rows, key_rows, value_rows, grad_rows, assignment, position):

time: 142 us -> 145 us (1.021)
  Pallas kernels: 9.9 us -> 12.1 us
    pallas_call x1, Pallas kernels: 9.9 us -> 12.1 us  [fused_attention(): pl.pallas_call(functools.partial(attention_kernel, block_rows=block_rows)...]
where the time goes in v7:
time: 145 us
  blocking collectives  110 us (76%)
  local copies, waits for them, and re-layouts  14 us (10%)
  Pallas kernels  12.1 us (8%)
  other arithmetic  5.32 us (4%)
  matrix products  2.35 us (2%)
    all_to_all x1, blocking collectives, shards(): lax.all_to_all(payload, order, 0, 0, tiled=True)  61.9 us
    all_to_all x1, blocking collectives, shards(): lax.all_to_all(all_slots, order, 0, 0, tiled=True)  48 us
    pallas_call x1, Pallas kernels, fused_attention(): pl.pallas_call(functools.partial(attention_kernel, block_rows=block_rows)...  12.1 us
    unnamed x12, local copies, waits for them, and re-layouts  3.49 us

profile of v7, /device:TPU:1, one launch (start us, length us, event | category | flops | bytes accessed | tf_op | source)
XLA Modules:
  0.0 144.6 jit_solution(12377601313883319348)
XLA Ops:
  0.6 0.0 copy-start
  0.6 0.0 copy-start.1
  0.7 0.0 copy-start.2
  0.7 0.0 copy-start.3
  0.7 0.1 eq.45
  0.8 0.9 bitcast_compare_fusion
  1.6 0.9 fusion.5
  2.6 0.7 add_bitcast_fusion
  3.3 0.3 fusion.1
  3.6 1.0 select_reduce_fusion
  4.5 0.1 select_n.31
  4.7 0.1 add_select_fusion.1
  4.8 0.1 copy.36
  4.9 0.1 copy.37
  5.0 0.1 copy.49
  5.1 0.0 copy-done
  5.2 0.0 copy-done.1
  5.2 0.1 copy_bitcast_fusion.2
  5.2 0.0 copy-done.2
  5.3 0.0 copy-done.3
  5.3 0.1 copy_bitcast_fusion
  5.3 0.6 convolution_convert_fusion
  5.9 1.2 copy.35
  7.2 2.2 %pad_maximum_fusion = bf16[256,13,2,128]{3,2,1,0:T(2,128)(2,1)S(1)} fusion(bf16[256,1,2,128]{3,2,1,0:T(2,128)(2,1)S(1)} %copy.49, bf16[256,12,2,128]{3,2,1,0:T(2,128)(2,1)S(1)} %bitcast.43), kind=kLoop, calls=%fused_computation | loop fusion | flops 851968 | bytes 3407872 | tf_op jit(solution)/shard_map/concatenate | solution.py:285
  9.4 61.9 %all_to_all.10 = bf16[256,13,2,128]{3,2,1,0:T(2,128)(2,1)S(1)} all-to-all(bf16[256,13,2,128]{3,2,1,0:T(2,128)(2,1)S(1)} %pad_maximum_fusion), channel_id=1, replica_groups=mesh['seq'=64,'head'=4] {'head','seq'}, dimensions={0} | all-to-all | bytes 3407872 | tf_op jit(solution)/shard_map/all_to_all | solution.py:289
  71.3 0.4 copy.39
  71.7 0.1 slice.35
  71.8 0.1 fusion.20
  71.9 0.7 reshape_reshape.6.place_ref
  72.7 1.1 reshape_reshape.8.place_col_ref
  73.8 1.0 copy.40
  74.8 2.3 %reshape.47.arrived_ref = bf16[1536,512]{1,0:T(8,128)(2,1)} reshape(bf16[256,24,128]{2,1,0:T(8,128)(2,1)S(1)} %copy.40) | data formatting | bytes 3145728 | tf_op jit(solution)/shard_map/reshape | solution.py:290
  77.0 12.1 %shard_map.93 = bf16[1536,512]{1,0:T(8,128)(2,1)} custom-call(s32[1,1536]{1,0:T(1,128)} %reshape_reshape.6.place_ref, s32[1536,1]{1,0:T(8,128)} %reshape_reshape.8.place_col_ref, bf16[1536,512]{1,0:T(8,128)(2,1)} %reshape.47.arrived_ref), custom_call_target="tpu_custom_call" | custom-call | tf_op jit(solution)/shard_map/pallas_call | solution.py:248
  89.2 2.4 %reshape.48 = bf16[256,6,4,128]{3,2,1,0:T(4,128)(2,1)S(1)} reshape(bf16[1536,512]{1,0:T(8,128)(2,1)} %shard_map.93) | data formatting | bytes 3145728 | tf_op jit(solution)/shard_map/reshape | solution.py:295
  91.5 48.0 %all_to_all.11 = bf16[256,6,4,128]{3,2,1,0:T(4,128)(2,1)S(1)} all-to-all(bf16[256,6,4,128]{3,2,1,0:T(4,128)(2,1)S(1)} %reshape.48), channel_id=1, replica_groups=mesh['seq'=64,'head'=4] {'head','seq'}, dimensions={0} | all-to-all | bytes 3145728 | tf_op jit(solution)/shard_map/all_to_all | solution.py:298
  139.5 0.6 reshape.49
  140.2 0.8 fusion.4
  141.0 0.1 fusion.25
  141.1 0.9 copy.53
  142.0 0.9 copy.52
  142.8 0.9 copy.51
  143.7 0.9 copy.50
  (6 shorter events, 0.1 us)
Async XLA Ops:
  0.6 4.5 %copy-start = (bf16[256,4,128]{2,1,0:T(4,128)(2,1)S(1)}, bf16[256,4,128]{2,1,0:T(4,128)(2,1)}, u32[]{:S(2)}) copy-start(bf16[256,4,128]{2,1,0:T(4,128)(2,1)} %param.7) | copy-start | bytes 786436
  0.6 4.5 %copy-start.1 = (bf16[256,4,128]{2,1,0:T(4,128)(2,1)S(1)}, bf16[256,4,128]{2,1,0:T(4,128)(2,1)}, u32[]{:S(2)}) copy-start(bf16[256,4,128]{2,1,0:T(4,128)(2,1)} %param.6) | copy-start | bytes 786436
  0.7 4.6 %copy-start.2 = (bf16[256,4,128]{2,1,0:T(4,128)(2,1)S(1)}, bf16[256,4,128]{2,1,0:T(4,128)(2,1)}, u32[]{:S(2)}) copy-start(bf16[256,4,128]{2,1,0:T(4,128)(2,1)} %param.9) | copy-start | bytes 786436
  0.7 4.6 %copy-start.3 = (bf16[256,4,128]{2,1,0:T(4,128)(2,1)S(1)}, bf16[256,4,128]{2,1,0:T(4,128)(2,1)}, u32[]{:S(2)}) copy-start(bf16[256,4,128]{2,1,0:T(4,128)(2,1)} %param.8) | copy-start | bytes 786436

commit v8 on v7

--- a/solution.py
+++ b/solution.py
@@ -243,7 +243,7 @@
     )
 
 
-def fused_attention(flat_place, arrived_flat, cluster_len, block_rows=128):
+def fused_attention(flat_place, arrived_flat, cluster_len, block_rows=256):
     slots, width = arrived_flat.shape
     return pl.pallas_call(
         functools.partial(attention_kernel, block_rows=block_rows),

time: 145 us -> 143 us (0.986)
  Pallas kernels: 12.1 us -> 10.2 us
    pallas_call x1, Pallas kernels: 12.1 us -> 10.2 us  [fused_attention(): pl.pallas_call(functools.partial(attention_kernel, block_rows=block_rows)...]
where the time goes in v8:
time: 143 us
  blocking collectives  110 us (77%)
  local copies, waits for them, and re-layouts  14 us (10%)
  Pallas kernels  10.2 us (7%)
  other arithmetic  5.32 us (4%)
  matrix products  2.35 us (2%)
    all_to_all x1, blocking collectives, shards(): lax.all_to_all(payload, order, 0, 0, tiled=True)  61.9 us
    all_to_all x1, blocking collectives, shards(): lax.all_to_all(all_slots, order, 0, 0, tiled=True)  48 us
    pallas_call x1, Pallas kernels, fused_attention(): pl.pallas_call(functools.partial(attention_kernel, block_rows=block_rows)...  10.2 us
    unnamed x12, local copies, waits for them, and re-layouts  3.49 us

profile of v8, /device:TPU:1, one launch (start us, length us, event | category | flops | bytes accessed | tf_op | source)
XLA Modules:
  0.0 142.6 jit_solution(12677258471027981593)
XLA Ops:
  0.6 0.0 copy-start
  0.6 0.0 copy-start.1
  0.7 0.0 copy-start.2
  0.7 0.0 copy-start.3
  0.7 0.1 eq.45
  0.8 0.9 bitcast_compare_fusion
  1.6 0.9 fusion.5
  2.6 0.7 add_bitcast_fusion
  3.3 0.3 fusion.1
  3.6 1.0 select_reduce_fusion
  4.5 0.1 select_n.31
  4.7 0.1 add_select_fusion.1
  4.8 0.1 copy.36
  4.9 0.1 copy.37
  5.0 0.1 copy.49
  5.1 0.0 copy-done
  5.2 0.0 copy-done.1
  5.2 0.1 copy_bitcast_fusion.2
  5.2 0.0 copy-done.2
  5.3 0.0 copy-done.3
  5.3 0.1 copy_bitcast_fusion
  5.3 0.6 convolution_convert_fusion
  5.9 1.2 copy.35
  7.2 2.2 %pad_maximum_fusion = bf16[256,13,2,128]{3,2,1,0:T(2,128)(2,1)S(1)} fusion(bf16[256,1,2,128]{3,2,1,0:T(2,128)(2,1)S(1)} %copy.49, bf16[256,12,2,128]{3,2,1,0:T(2,128)(2,1)S(1)} %bitcast.43), kind=kLoop, calls=%fused_computation | loop fusion | flops 851968 | bytes 3407872 | tf_op jit(solution)/shard_map/concatenate | solution.py:285
  9.4 61.9 %all_to_all.10 = bf16[256,13,2,128]{3,2,1,0:T(2,128)(2,1)S(1)} all-to-all(bf16[256,13,2,128]{3,2,1,0:T(2,128)(2,1)S(1)} %pad_maximum_fusion), channel_id=1, replica_groups=mesh['seq'=64,'head'=4] {'head','seq'}, dimensions={0} | all-to-all | bytes 3407872 | tf_op jit(solution)/shard_map/all_to_all | solution.py:289
  71.3 0.4 copy.39
  71.7 0.1 slice.35
  71.8 0.1 fusion.20
  71.9 0.7 reshape_reshape.6.place_ref
  72.7 1.1 reshape_reshape.8.place_col_ref
  73.8 1.0 copy.40
  74.8 2.3 %reshape.47.arrived_ref = bf16[1536,512]{1,0:T(8,128)(2,1)} reshape(bf16[256,24,128]{2,1,0:T(8,128)(2,1)S(1)} %copy.40) | data formatting | bytes 3145728 | tf_op jit(solution)/shard_map/reshape | solution.py:290
  77.0 10.2 %shard_map.93 = bf16[1536,512]{1,0:T(8,128)(2,1)} custom-call(s32[1,1536]{1,0:T(1,128)} %reshape_reshape.6.place_ref, s32[1536,1]{1,0:T(8,128)} %reshape_reshape.8.place_col_ref, bf16[1536,512]{1,0:T(8,128)(2,1)} %reshape.47.arrived_ref), custom_call_target="tpu_custom_call" | custom-call | tf_op jit(solution)/shard_map/pallas_call | solution.py:248
  87.2 2.4 %reshape.48 = bf16[256,6,4,128]{3,2,1,0:T(4,128)(2,1)S(1)} reshape(bf16[1536,512]{1,0:T(8,128)(2,1)} %shard_map.93) | data formatting | bytes 3145728 | tf_op jit(solution)/shard_map/reshape | solution.py:295
  89.6 48.0 %all_to_all.11 = bf16[256,6,4,128]{3,2,1,0:T(4,128)(2,1)S(1)} all-to-all(bf16[256,6,4,128]{3,2,1,0:T(4,128)(2,1)S(1)} %reshape.48), channel_id=1, replica_groups=mesh['seq'=64,'head'=4] {'head','seq'}, dimensions={0} | all-to-all | bytes 3145728 | tf_op jit(solution)/shard_map/all_to_all | solution.py:298
  137.6 0.6 reshape.49
  138.2 0.8 fusion.4
  139.0 0.1 fusion.25
  139.1 0.9 copy.53
  140.0 0.9 copy.52
  140.9 0.9 copy.51
  141.7 0.9 copy.50
  (6 shorter events, 0.1 us)
Async XLA Ops:
  0.6 4.5 %copy-start = (bf16[256,4,128]{2,1,0:T(4,128)(2,1)S(1)}, bf16[256,4,128]{2,1,0:T(4,128)(2,1)}, u32[]{:S(2)}) copy-start(bf16[256,4,128]{2,1,0:T(4,128)(2,1)} %param.7) | copy-start | bytes 786436
  0.6 4.5 %copy-start.1 = (bf16[256,4,128]{2,1,0:T(4,128)(2,1)S(1)}, bf16[256,4,128]{2,1,0:T(4,128)(2,1)}, u32[]{:S(2)}) copy-start(bf16[256,4,128]{2,1,0:T(4,128)(2,1)} %param.6) | copy-start | bytes 786436
  0.7 4.6 %copy-start.2 = (bf16[256,4,128]{2,1,0:T(4,128)(2,1)S(1)}, bf16[256,4,128]{2,1,0:T(4,128)(2,1)}, u32[]{:S(2)}) copy-start(bf16[256,4,128]{2,1,0:T(4,128)(2,1)} %param.9) | copy-start | bytes 786436
  0.7 4.6 %copy-start.3 = (bf16[256,4,128]{2,1,0:T(4,128)(2,1)S(1)}, bf16[256,4,128]{2,1,0:T(4,128)(2,1)}, u32[]{:S(2)}) copy-start(bf16[256,4,128]{2,1,0:T(4,128)(2,1)} %param.8) | copy-start | bytes 786436

commit v9 on v6

--- a/solution.py
+++ b/solution.py
@@ -240,7 +240,7 @@
     ).astype(jnp.bfloat16)
 
 
-def fused_attention(flat_place, arrived_flat, cluster_len, block_rows=256):
+def fused_attention(flat_place, arrived_flat, cluster_len, block_rows=512):
     slots, width = arrived_flat.shape
     return pl.pallas_call(
         functools.partial(attention_kernel, block_rows=block_rows),

time: 142 us -> 142 us (level)
  no operation moved by 1% of the time
where the time goes in v9:
time: 142 us; the launch traced here: 141 us
  blocking collectives  110 us (77%)
  local copies, waits for them, and re-layouts  12.9 us (9%)
  Pallas kernels  10.1 us (7%)
  other arithmetic  5.32 us (4%)
  matrix products  2.35 us (2%)
    all_to_all x1, blocking collectives, shards(): lax.all_to_all(payload, order, 0, 0, tiled=True)  61.9 us
    all_to_all x1, blocking collectives, shards(): lax.all_to_all(all_slots, order, 0, 0, tiled=True)  48 us
    pallas_call x1, Pallas kernels, fused_attention(): pl.pallas_call(functools.partial(attention_kernel, block_rows=block_rows)...  10.1 us
    unnamed x12, local copies, waits for them, and re-layouts  3.49 us

profile of v9, /device:TPU:1, one launch (start us, length us, event | category | flops | bytes accessed | tf_op | source)
XLA Modules:
  0.0 141.4 jit_solution(13179271213820368296)
XLA Ops:
  0.6 0.0 copy-start
  0.6 0.0 copy-start.1
  0.7 0.0 copy-start.2
  0.7 0.0 copy-start.3
  0.7 0.1 eq.45
  0.8 0.9 bitcast_compare_fusion
  1.6 0.9 fusion.5
  2.6 0.7 add_bitcast_fusion
  3.3 0.3 fusion.1
  3.6 1.0 select_reduce_fusion
  4.5 0.1 select_n.31
  4.7 0.1 add_select_fusion.1
  4.8 0.1 copy.35
  4.9 0.1 copy.36
  5.0 0.1 copy.47
  5.1 0.0 copy-done
  5.2 0.0 copy-done.1
  5.2 0.1 copy_bitcast_fusion.2
  5.2 0.0 copy-done.2
  5.3 0.0 copy-done.3
  5.3 0.1 copy_bitcast_fusion
  5.3 0.6 convolution_convert_fusion
  5.9 1.2 copy.34
  7.2 2.2 %pad_maximum_fusion = bf16[256,13,2,128]{3,2,1,0:T(2,128)(2,1)S(1)} fusion(bf16[256,1,2,128]{3,2,1,0:T(2,128)(2,1)S(1)} %copy.47, bf16[256,12,2,128]{3,2,1,0:T(2,128)(2,1)S(1)} %bitcast.43), kind=kLoop, calls=%fused_computation | loop fusion | flops 851968 | bytes 3407872 | tf_op jit(solution)/shard_map/concatenate | solution.py:282
  9.4 61.9 %all_to_all.10 = bf16[256,13,2,128]{3,2,1,0:T(2,128)(2,1)S(1)} all-to-all(bf16[256,13,2,128]{3,2,1,0:T(2,128)(2,1)S(1)} %pad_maximum_fusion), channel_id=1, replica_groups=mesh['seq'=64,'head'=4] {'head','seq'}, dimensions={0} | all-to-all | bytes 3407872 | tf_op jit(solution)/shard_map/all_to_all | solution.py:286
  71.3 0.4 copy.38
  71.7 0.1 slice.35
  71.8 1.0 copy.39
  72.8 2.3 %reshape.47.arrived_ref = bf16[1536,512]{1,0:T(8,128)(2,1)} reshape(bf16[256,24,128]{2,1,0:T(8,128)(2,1)S(1)} %copy.39) | data formatting | bytes 3145728 | tf_op jit(solution)/shard_map/reshape | solution.py:287
  75.1 0.1 fusion.20
  75.2 0.7 reshape_reshape.3.place_ref
  75.9 10.1 %shard_map.93 = bf16[1536,512]{1,0:T(8,128)(2,1)} custom-call(s32[1,1536]{1,0:T(1,128)} %reshape_reshape.3.place_ref, bf16[1536,512]{1,0:T(8,128)(2,1)} %reshape.47.arrived_ref), custom_call_target="tpu_custom_call" | custom-call | tf_op jit(solution)/shard_map/pallas_call | solution.py:245
  86.0 2.4 %reshape.48 = bf16[256,6,4,128]{3,2,1,0:T(4,128)(2,1)S(1)} reshape(bf16[1536,512]{1,0:T(8,128)(2,1)} %shard_map.93) | data formatting | bytes 3145728 | tf_op jit(solution)/shard_map/reshape | solution.py:292
  88.4 48.0 %all_to_all.11 = bf16[256,6,4,128]{3,2,1,0:T(4,128)(2,1)S(1)} all-to-all(bf16[256,6,4,128]{3,2,1,0:T(4,128)(2,1)S(1)} %reshape.48), channel_id=1, replica_groups=mesh['seq'=64,'head'=4] {'head','seq'}, dimensions={0} | all-to-all | bytes 3145728 | tf_op jit(solution)/shard_map/all_to_all | solution.py:295
  136.4 0.6 reshape.49
  137.0 0.8 fusion.4
  137.8 0.1 fusion.25
  137.9 0.9 copy.51
  138.8 0.9 copy.50
  139.6 0.9 copy.49
  140.5 0.9 copy.48
  (6 shorter events, 0.1 us)
Async XLA Ops:
  0.6 4.5 %copy-start = (bf16[256,4,128]{2,1,0:T(4,128)(2,1)S(1)}, bf16[256,4,128]{2,1,0:T(4,128)(2,1)}, u32[]{:S(2)}) copy-start(bf16[256,4,128]{2,1,0:T(4,128)(2,1)} %param.7) | copy-start | bytes 786436
  0.6 4.5 %copy-start.1 = (bf16[256,4,128]{2,1,0:T(4,128)(2,1)S(1)}, bf16[256,4,128]{2,1,0:T(4,128)(2,1)}, u32[]{:S(2)}) copy-start(bf16[256,4,128]{2,1,0:T(4,128)(2,1)} %param.6) | copy-start | bytes 786436
  0.7 4.6 %copy-start.2 = (bf16[256,4,128]{2,1,0:T(4,128)(2,1)S(1)}, bf16[256,4,128]{2,1,0:T(4,128)(2,1)}, u32[]{:S(2)}) copy-start(bf16[256,4,128]{2,1,0:T(4,128)(2,1)} %param.9) | copy-start | bytes 786436
  0.7 4.6 %copy-start.3 = (bf16[256,4,128]{2,1,0:T(4,128)(2,1)S(1)}, bf16[256,4,128]{2,1,0:T(4,128)(2,1)}, u32[]{:S(2)}) copy-start(bf16[256,4,128]{2,1,0:T(4,128)(2,1)} %param.8) | copy-start | bytes 786436

commit v10 on v6

--- a/solution.py
+++ b/solution.py
@@ -293,12 +293,19 @@
         devices, capacity, 4, head_width
     )
     returned = lax.all_to_all(all_slots, order, 0, 0, tiled=True).reshape(
-        head_count, slot_count, 4 * head_width
-    )
-    everything = jnp.einsum(
-        "hsr,hsf->rhf", hits_low, returned, preferred_element_type=jnp.float32
-    ).astype(jnp.bfloat16).reshape(sub_rows, head_count, 4, head_width)
-    return (everything[:, :, 0], everything[:, :, 1], everything[:, :, 2], everything[:, :, 3])
+        devices * capacity, 4 * head_width
+    )
+    back_target = (jnp.arange(head_count, dtype=jnp.int32)[None, :] * slot_count + local_slot).reshape(-1)
+    back_hits = (
+        jnp.arange(devices * capacity, dtype=jnp.int32)[None, :] == back_target[:, None]
+    ).astype(jnp.bfloat16)
+    everything = jnp.dot(back_hits, returned, preferred_element_type=jnp.float32)
+    return tuple(
+        everything[:, member * head_width : (member + 1) * head_width]
+        .astype(jnp.bfloat16)
+        .reshape(sub_rows, head_count, head_width)
+        for member in range(4)
+    )
 
 
 def solution(mesh):

time: 142 us -> 141 us (level)
  blocking collectives: 110 us -> 61.9 us
  waiting for transfers between devices: 0 us -> 42.8 us
  starting transfers between devices: 0 us -> 5.18 us
  local copies, waits for them, and re-layouts: 12.9 us -> 11.2 us
    all_to_all x1 -> x0, blocking collectives: 48 us -> none  [shards(): lax.all_to_all(all_slots, order, 0, 0, tiled=True)]
    all_to_all x0 -> x1, waiting for transfers between devices: none -> 42.8 us  [shards(): lax.all_to_all(all_slots, order, 0, 0, tiled=True)]
    all_to_all x0 -> x1, starting transfers between devices: none -> 5.18 us  [shards(): lax.all_to_all(all_slots, order, 0, 0, tiled=True)]
    unnamed x12 -> x8, local copies, waits for them, and re-layouts: 3.49 us -> 0.02 us
  transfers between devices with their start and end apart: 0 -> 1, of which waited for: 0 -> 1; matrix products, arithmetic and copies ran while one was open for 0% -> 0% of each run, Pallas kernels for 0% -> 0%
where the time goes in v10:
time: 141 us
  blocking collectives  61.9 us (44%)
  waiting for transfers between devices  42.8 us (30%)
  local copies, waits for them, and re-layouts  11.2 us (8%)
  Pallas kernels  9.92 us (7%)
  other arithmetic  5.39 us (4%)
  starting transfers between devices  5.18 us (4%)
  matrix products  3.35 us (2%)
    all_to_all x1, blocking collectives, shards(): lax.all_to_all(payload, order, 0, 0, tiled=True)  61.9 us
    all_to_all x1, waiting for transfers between devices, shards(): lax.all_to_all(all_slots, order, 0, 0, tiled=True)  42.8 us
    pallas_call x1, Pallas kernels, fused_attention(): pl.pallas_call(functools.partial(attention_kernel, block_rows=block_rows)...  9.92 us
    all_to_all x1, starting transfers between devices, shards(): lax.all_to_all(all_slots, order, 0, 0, tiled=True)  5.18 us
    reshape x1, local copies, waits for them, and re-layouts, shards(): fused_attention(flat_place, arrived_data, cluster_len)  3.5 us
  transfers between devices with their start and end apart: 1, of which 1 were waited for; matrix products, arithmetic and copies ran while one was open for 0% of the time, Pallas kernels for 0%

profile of v10, /device:TPU:1, one launch (start us, length us, event | category | flops | bytes accessed | tf_op | source)
XLA Modules:
  0.0 140.5 jit_solution(303737598942453097)
XLA Ops:
  0.6 0.0 copy-start
  0.6 0.0 copy-start.1
  0.7 0.0 copy-start.2
  0.7 0.0 copy-start.3
  0.7 0.1 eq.60
  0.8 0.9 bitcast_compare_fusion
  1.6 0.9 fusion.10
  2.6 0.8 broadcast_add_fusion
  3.3 0.3 fusion.4
  3.6 1.0 select_reduce_fusion
  4.6 0.1 select_n.31
  4.8 0.1 add_select_fusion.1
  4.9 0.1 copy.28
  5.0 0.1 copy.29
  5.1 0.1 copy.34
  5.2 0.0 copy-done
  5.2 0.0 copy-done.1
  5.2 0.1 copy_bitcast_fusion.2
  5.3 0.0 copy-done.2
  5.3 0.0 copy-done.3
  5.3 0.1 copy_bitcast_fusion
  5.4 0.6 convolution_convert_fusion
  6.0 1.2 copy.27
  7.2 2.2 %pad_maximum_fusion = bf16[256,13,2,128]{3,2,1,0:T(2,128)(2,1)S(1)} fusion(bf16[256,1,2,128]{3,2,1,0:T(2,128)(2,1)S(1)} %copy.34, bf16[256,12,2,128]{3,2,1,0:T(2,128)(2,1)S(1)} %bitcast.46), kind=kLoop, calls=%fused_computation.3 | loop fusion | flops 851968 | bytes 3407872 | tf_op jit(solution)/shard_map/concatenate | solution.py:282
  9.5 61.9 %all_to_all.10 = bf16[256,13,2,128]{3,2,1,0:T(2,128)(2,1)S(1)} all-to-all(bf16[256,13,2,128]{3,2,1,0:T(2,128)(2,1)S(1)} %pad_maximum_fusion), channel_id=1, replica_groups=mesh['seq'=64,'head'=4] {'head','seq'}, dimensions={0} | all-to-all | bytes 3407872 | tf_op jit(solution)/shard_map/all_to_all | solution.py:286
  71.4 0.4 copy.31
  71.8 0.1 slice.39
  71.9 1.0 copy.32
  72.9 2.2 %reshape.62.arrived_ref = bf16[1536,512]{1,0:T(8,128)(2,1)} reshape(bf16[256,24,128]{2,1,0:T(8,128)(2,1)S(1)} %copy.32) | data formatting | bytes 3145728 | tf_op jit(solution)/shard_map/reshape | solution.py:287
  75.2 0.1 fusion.24
  75.3 0.7 reshape_reshape.3.place_ref
  76.0 9.9 %shard_map.93 = bf16[1536,512]{1,0:T(8,128)(2,1)} custom-call(s32[1,1536]{1,0:T(1,128)} %reshape_reshape.3.place_ref, bf16[1536,512]{1,0:T(8,128)(2,1)} %reshape.62.arrived_ref), custom_call_target="tpu_custom_call" | custom-call | tf_op jit(solution)/shard_map/pallas_call | solution.py:245
  85.9 3.5 %reshape.63 = bf16[256,6,4,128]{3,2,1,0:T(4,128)(2,1)} reshape(bf16[1536,512]{1,0:T(8,128)(2,1)} %shard_map.93) | data formatting | bytes 3145728 | tf_op jit(solution)/shard_map/reshape | solution.py:292
  89.4 5.2 %all-to-all-start.1 = ((bf16[256,6,4,128]{3,2,1,0:T(4,128)(2,1)}), bf16[256,6,4,128]{3,2,1,0:T(4,128)(2,1)S(1)}, u32[]{:S(2)}, u32[]{:S(2)}) async-start(bf16[256,6,4,128]{3,2,1,0:T(4,128)(2,1)} %reshape.63), calls=%async_computation.1 | async-start | bytes 3145728 | tf_op jit(solution)/shard_map/all_to_all | solution.py:295
  94.6 0.1 copy.22
  94.8 0.1 eq.63
  94.9 42.8 %all-to-all-done.1 = bf16[256,6,4,128]{3,2,1,0:T(4,128)(2,1)S(1)} async-done(((bf16[256,6,4,128]{3,2,1,0:T(4,128)(2,1)}), bf16[256,6,4,128]{3,2,1,0:T(4,128)(2,1)S(1)}, u32[]{:S(2)}, u32[]{:S(2)}) %all-to-all-start.1) | async-done | bytes 1572896 | tf_op jit(solution)/shard_map/all_to_all | solution.py:295
  137.6 1.8 %fusion.7 = bf16[1024,512]{1,0:T(8,128)(2,1)S(1)} fusion(bf16[192,8,4,128]{3,2,1,0:T(4,128)(2,1)S(1)} %bitcast.47, s32[1024]{0:T(1024)S(1)} %eq.63), kind=kOutput, calls=%fused_computation.11 | convolution fusion | flops 1612709888 | bytes 2625536 | tf_op jit(solution)/shard_map/dot_general | solution.py:302
  139.5 1.1 fusion.30
  (7 shorter events, 0.1 us)
Async XLA Ops:
  0.6 4.6 %copy-start = (bf16[256,4,128]{2,1,0:T(4,128)(2,1)S(1)}, bf16[256,4,128]{2,1,0:T(4,128)(2,1)}, u32[]{:S(2)}) copy-start(bf16[256,4,128]{2,1,0:T(4,128)(2,1)} %param.7) | copy-start | bytes 786436
  0.6 4.6 %copy-start.1 = (bf16[256,4,128]{2,1,0:T(4,128)(2,1)S(1)}, bf16[256,4,128]{2,1,0:T(4,128)(2,1)}, u32[]{:S(2)}) copy-start(bf16[256,4,128]{2,1,0:T(4,128)(2,1)} %param.6) | copy-start | bytes 786436
  0.7 4.7 %copy-start.2 = (bf16[256,4,128]{2,1,0:T(4,128)(2,1)S(1)}, bf16[256,4,128]{2,1,0:T(4,128)(2,1)}, u32[]{:S(2)}) copy-start(bf16[256,4,128]{2,1,0:T(4,128)(2,1)} %param.9) | copy-start | bytes 786436
  0.7 4.7 %copy-start.3 = (bf16[256,4,128]{2,1,0:T(4,128)(2,1)S(1)}, bf16[256,4,128]{2,1,0:T(4,128)(2,1)}, u32[]{:S(2)}) copy-start(bf16[256,4,128]{2,1,0:T(4,128)(2,1)} %param.8) | copy-start | bytes 786436
  89.4 48.2 %all-to-all-start.1 = ((bf16[256,6,4,128]{3,2,1,0:T(4,128)(2,1)}), bf16[256,6,4,128]{3,2,1,0:T(4,128)(2,1)S(1)}, u32[]{:S(2)}, u32[]{:S(2)}) async-start(bf16[256,6,4,128]{3,2,1,0:T(4,128)(2,1)} %reshape.63), calls=%async_computation.1 | async-start | bytes 3145728 | tf_op jit(solution)/shard_map/all_to_all | solution.py:295

commit v11 on v10

--- a/solution.py
+++ b/solution.py
@@ -235,16 +235,20 @@
         )
     y_ref[:, 2 * head_width : 3 * head_width] = (dk_acc[...] * scale).astype(jnp.bfloat16)
     y_ref[:, 3 * head_width : 4 * head_width] = dv_acc[...].astype(jnp.bfloat16)
-    out_ref[...] = lax.dot_general(
+    result = lax.dot_general(
         order, y_ref[...], (((0,), (0,)), ((), ())), preferred_element_type=jnp.float32
-    ).astype(jnp.bfloat16)
+    )
+    for member in range(4):
+        out_ref[pl.ds(member, place_ref.shape[1], stride=4), :] = result[
+            :, member * head_width : (member + 1) * head_width
+        ]
 
 
 def fused_attention(flat_place, arrived_flat, cluster_len, block_rows=256):
     slots, width = arrived_flat.shape
     return pl.pallas_call(
         functools.partial(attention_kernel, block_rows=block_rows),
-        out_shape=jax.ShapeDtypeStruct((slots, width), jnp.bfloat16),
+        out_shape=jax.ShapeDtypeStruct((slots * 4, width // 4), jnp.float32),
         scratch_shapes=[
             pltpu.VMEM((cluster_len, width), jnp.bfloat16),
             pltpu.VMEM((cluster_len, width), jnp.bfloat16),
@@ -289,8 +293,10 @@
     flat_place = (
         arrived_code[:, :capacity] * 32.0 + arrived_code[:, capacity : 2 * capacity]
     ).astype(jnp.int32).reshape(-1)
-    all_slots = fused_attention(flat_place, arrived_data, cluster_len).reshape(
-        devices, capacity, 4, head_width
+    all_slots = (
+        fused_attention(flat_place, arrived_data, cluster_len)
+        .astype(jnp.bfloat16)
+        .reshape(devices, capacity, 4, head_width)
     )
     returned = lax.all_to_all(all_slots, order, 0, 0, tiled=True).reshape(
         devices * capacity, 4 * head_width

time: 141 us -> 141 us (level)
  local copies, waits for them, and re-layouts: 11.2 us -> 7.64 us
  other arithmetic: 5.39 us -> 8.58 us
    reshape x1 -> x0, local copies, waits for them, and re-layouts: 3.5 us -> none  [shards(): fused_attention(flat_place, arrived_data, cluster_len)]
    convert_element_type x0 -> x1, other arithmetic: none -> 3.19 us  [shards(): all_slots = fused_attention(flat_place, arrived_data, cluster_len).astype...]
where the time goes in v11:
time: 141 us
  blocking collectives  61.9 us (44%)
  waiting for transfers between devices  42.8 us (30%)
  Pallas kernels  10.4 us (7%)
  other arithmetic  8.58 us (6%)
  local copies, waits for them, and re-layouts  7.64 us (5%)
  starting transfers between devices  5.18 us (4%)
  matrix products  3.35 us (2%)
    all_to_all x1, blocking collectives, shards(): lax.all_to_all(payload, order, 0, 0, tiled=True)  61.9 us
    all_to_all x1, waiting for transfers between devices, shards(): lax.all_to_all(all_slots, order, 0, 0, tiled=True)  42.8 us
    pallas_call x1, Pallas kernels, fused_attention(): pl.pallas_call(functools.partial(attention_kernel, block_rows=block_rows)...  10.4 us
    all_to_all x1, starting transfers between devices, shards(): lax.all_to_all(all_slots, order, 0, 0, tiled=True)  5.18 us
    convert_element_type x1, other arithmetic, shards(): all_slots = fused_attention(flat_place, arrived_data, cluster_len).astype...  3.19 us
  transfers between devices with their start and end apart: 1, of which 1 were waited for; matrix products, arithmetic and copies ran while one was open for 0% of the time, Pallas kernels for 0%

profile of v11, /device:TPU:1, one launch (start us, length us, event | category | flops | bytes accessed | tf_op | source)
XLA Modules:
  0.0 140.7 jit_solution(3792177737063465298)
XLA Ops:
  0.6 0.0 copy-start
  0.6 0.0 copy-start.1
  0.7 0.0 copy-start.2
  0.7 0.0 copy-start.3
  0.7 0.1 eq.60
  0.8 0.9 bitcast_compare_fusion
  1.6 0.9 fusion.10
  2.6 0.8 broadcast_add_fusion
  3.3 0.3 fusion.4
  3.6 1.0 select_reduce_fusion
  4.6 0.1 select_n.31
  4.8 0.1 add_select_fusion.1
  4.9 0.1 copy.28
  5.0 0.1 copy.29
  5.1 0.1 copy.34
  5.2 0.0 copy-done
  5.2 0.0 copy-done.1
  5.2 0.1 copy_bitcast_fusion.2
  5.3 0.0 copy-done.2
  5.3 0.0 copy-done.3
  5.3 0.1 copy_bitcast_fusion
  5.4 0.6 convolution_convert_fusion
  6.0 1.2 copy.27
  7.2 2.2 %pad_maximum_fusion = bf16[256,13,2,128]{3,2,1,0:T(2,128)(2,1)S(1)} fusion(bf16[256,1,2,128]{3,2,1,0:T(2,128)(2,1)S(1)} %copy.34, bf16[256,12,2,128]{3,2,1,0:T(2,128)(2,1)S(1)} %bitcast.47), kind=kLoop, calls=%fused_computation.3 | loop fusion | flops 851968 | bytes 3407872 | tf_op jit(solution)/shard_map/concatenate | solution.py:286
  9.5 61.9 %all_to_all.10 = bf16[256,13,2,128]{3,2,1,0:T(2,128)(2,1)S(1)} all-to-all(bf16[256,13,2,128]{3,2,1,0:T(2,128)(2,1)S(1)} %pad_maximum_fusion), channel_id=1, replica_groups=mesh['seq'=64,'head'=4] {'head','seq'}, dimensions={0} | all-to-all | bytes 3407872 | tf_op jit(solution)/shard_map/all_to_all | solution.py:290
  71.4 0.4 copy.31
  71.8 0.1 slice.39
  71.9 1.0 copy.32
  72.9 2.2 %reshape.62.arrived_ref = bf16[1536,512]{1,0:T(8,128)(2,1)} reshape(bf16[256,24,128]{2,1,0:T(8,128)(2,1)S(1)} %copy.32) | data formatting | bytes 3145728 | tf_op jit(solution)/shard_map/reshape | solution.py:291
  75.1 0.1 fusion.24
  75.2 0.7 reshape_reshape.3.place_ref
  76.0 10.4 %shard_map.93 = f32[6144,128]{1,0:T(8,128)} custom-call(s32[1,1536]{1,0:T(1,128)} %reshape_reshape.3.place_ref, bf16[1536,512]{1,0:T(8,128)(2,1)} %reshape.62.arrived_ref), custom_call_target="tpu_custom_call" | custom-call | tf_op jit(solution)/shard_map/pallas_call | solution.py:249
  86.4 3.2 %convert_element_type.34 = bf16[6144,128]{1,0:T(8,128)(2,1)} convert(f32[6144,128]{1,0:T(8,128)} %shard_map.93) | non-fusion elementwise | flops 786432 | bytes 4718592 | tf_op jit(solution)/shard_map/convert_element_type | solution.py:298
  89.6 5.2 %all-to-all-start.1 = ((bf16[256,6,4,128]{3,2,1,0:T(4,128)(2,1)}), bf16[256,6,4,128]{3,2,1,0:T(4,128)(2,1)S(1)}, u32[]{:S(2)}, u32[]{:S(2)}) async-start(bf16[256,6,4,128]{3,2,1,0:T(4,128)(2,1)} %bitcast.17), calls=%async_computation.1 | async-start | bytes 3145728 | tf_op jit(solution)/shard_map/all_to_all | solution.py:301
  94.8 0.1 copy.22
  94.9 0.1 eq.63
  95.0 42.8 %all-to-all-done.1 = bf16[256,6,4,128]{3,2,1,0:T(4,128)(2,1)S(1)} async-done(((bf16[256,6,4,128]{3,2,1,0:T(4,128)(2,1)}), bf16[256,6,4,128]{3,2,1,0:T(4,128)(2,1)S(1)}, u32[]{:S(2)}, u32[]{:S(2)}) %all-to-all-start.1) | async-done | bytes 1572896 | tf_op jit(solution)/shard_map/all_to_all | solution.py:301
  137.8 1.8 %fusion.7 = bf16[1024,512]{1,0:T(8,128)(2,1)S(1)} fusion(bf16[192,8,4,128]{3,2,1,0:T(4,128)(2,1)S(1)} %bitcast.48, s32[1024]{0:T(1024)S(1)} %eq.63), kind=kOutput, calls=%fused_computation.11 | convolution fusion | flops 1612709888 | bytes 2625536 | tf_op jit(solution)/shard_map/dot_general | solution.py:308
  139.6 1.1 fusion.30
  (7 shorter events, 0.1 us)
Async XLA Ops:
  0.6 4.6 %copy-start = (bf16[256,4,128]{2,1,0:T(4,128)(2,1)S(1)}, bf16[256,4,128]{2,1,0:T(4,128)(2,1)}, u32[]{:S(2)}) copy-start(bf16[256,4,128]{2,1,0:T(4,128)(2,1)} %param.7) | copy-start | bytes 786436
  0.6 4.6 %copy-start.1 = (bf16[256,4,128]{2,1,0:T(4,128)(2,1)S(1)}, bf16[256,4,128]{2,1,0:T(4,128)(2,1)}, u32[]{:S(2)}) copy-start(bf16[256,4,128]{2,1,0:T(4,128)(2,1)} %param.6) | copy-start | bytes 786436
  0.7 4.7 %copy-start.2 = (bf16[256,4,128]{2,1,0:T(4,128)(2,1)S(1)}, bf16[256,4,128]{2,1,0:T(4,128)(2,1)}, u32[]{:S(2)}) copy-start(bf16[256,4,128]{2,1,0:T(4,128)(2,1)} %param.9) | copy-start | bytes 786436
  0.7 4.7 %copy-start.3 = (bf16[256,4,128]{2,1,0:T(4,128)(2,1)S(1)}, bf16[256,4,128]{2,1,0:T(4,128)(2,1)}, u32[]{:S(2)}) copy-start(bf16[256,4,128]{2,1,0:T(4,128)(2,1)} %param.8) | copy-start | bytes 786436
  89.6 48.2 %all-to-all-start.1 = ((bf16[256,6,4,128]{3,2,1,0:T(4,128)(2,1)}), bf16[256,6,4,128]{3,2,1,0:T(4,128)(2,1)S(1)}, u32[]{:S(2)}, u32[]{:S(2)}) async-start(bf16[256,6,4,128]{3,2,1,0:T(4,128)(2,1)} %bitcast.17), calls=%async_computation.1 | async-start | bytes 3145728 | tf_op jit(solution)/shard_map/all_to_all | solution.py:301

commit v12 on v11

--- a/solution.py
+++ b/solution.py
@@ -272,7 +272,10 @@
     hits_low = hits.astype(jnp.bfloat16)
     stacked = jnp.stack((query_rows, key_rows, value_rows, grad_rows), axis=2)
     packed = jnp.einsum(
-        "hsr,rhaf->hsaf", hits_low, stacked, preferred_element_type=jnp.float32
+        "hsr,rhf->hsf",
+        hits_low,
+        stacked.reshape(sub_rows, head_count, 4 * head_width),
+        preferred_element_type=jnp.float32,
     ).astype(jnp.bfloat16)
     places = jnp.where(
         jnp.any(hits, axis=2),

time: 141 us -> 142 us (level)
  no operation moved by 1% of the time
where the time goes in v12:
time: 142 us
  blocking collectives  61.9 us (44%)
  waiting for transfers between devices  42.8 us (30%)
  Pallas kernels  10.4 us (7%)
  other arithmetic  9.54 us (7%)
  local copies, waits for them, and re-layouts  7.95 us (6%)
  starting transfers between devices  5.18 us (4%)
  matrix products  3.34 us (2%)
    all_to_all x1, blocking collectives, shards(): lax.all_to_all(payload, order, 0, 0, tiled=True)  61.9 us
    all_to_all x1, waiting for transfers between devices, shards(): lax.all_to_all(all_slots, order, 0, 0, tiled=True)  42.8 us
    pallas_call x1, Pallas kernels, fused_attention(): pl.pallas_call(functools.partial(attention_kernel, block_rows=block_rows)...  10.4 us
    all_to_all x1, starting transfers between devices, shards(): lax.all_to_all(all_slots, order, 0, 0, tiled=True)  5.18 us
    convert_element_type x1, other arithmetic, shards(): all_slots = fused_attention(flat_place, arrived_data, cluster_len).astype...  3.19 us
  transfers between devices with their start and end apart: 1, of which 1 were waited for; matrix products, arithmetic and copies ran while one was open for 0% of the time, Pallas kernels for 0%

profile of v12, /device:TPU:1, one launch (start us, length us, event | category | flops | bytes accessed | tf_op | source)
XLA Modules:
  0.0 142.0 jit_solution(13069986383330216120)
XLA Ops:
  0.6 0.0 copy-start
  0.6 0.0 copy-start.1
  0.7 0.0 copy-start.2
  0.7 0.0 copy-start.3
  0.7 0.1 eq.60
  0.8 0.9 bitcast_compare_fusion
  1.6 0.9 fusion.8
  2.6 0.8 broadcast_add_fusion
  3.3 0.3 fusion.4
  3.6 1.0 select_reduce_fusion
  4.6 0.1 select_n.31
  4.8 0.1 add_select_fusion.1
  4.9 0.1 copy.18
  5.0 0.1 copy.19
  5.1 0.1 copy.23
  5.2 0.0 copy-done
  5.2 0.0 copy-done.1
  5.2 0.0 copy-done.2
  5.3 0.0 copy-done.3
  5.3 1.0 pad_maximum_fusion.1
  6.2 0.8 copy.17
  7.0 0.4 reshape.62
  7.5 0.6 convolution_convert_fusion
  8.1 0.4 reshape.63
  8.5 2.2 %pad_maximum_fusion = bf16[256,13,2,128]{3,2,1,0:T(2,128)(2,1)S(1)} fusion(bf16[256,1,2,128]{3,2,1,0:T(2,128)(2,1)S(1)} %copy.23, bf16[256,12,2,128]{3,2,1,0:T(2,128)(2,1)S(1)} %reshape.63), kind=kLoop, calls=%fused_computation.3 | loop fusion | flops 851968 | bytes 3407872 | tf_op jit(solution)/shard_map/concatenate | solution.py:289
  10.7 61.9 %all_to_all.10 = bf16[256,13,2,128]{3,2,1,0:T(2,128)(2,1)S(1)} all-to-all(bf16[256,13,2,128]{3,2,1,0:T(2,128)(2,1)S(1)} %pad_maximum_fusion), channel_id=1, replica_groups=mesh['seq'=64,'head'=4] {'head','seq'}, dimensions={0} | all-to-all | bytes 3407872 | tf_op jit(solution)/shard_map/all_to_all | solution.py:293
  72.7 0.4 copy.21
  73.0 0.1 slice.39
  73.2 1.0 copy.22
  74.2 2.2 %reshape.66.arrived_ref = bf16[1536,512]{1,0:T(8,128)(2,1)} reshape(bf16[256,24,128]{2,1,0:T(8,128)(2,1)S(1)} %copy.22) | data formatting | bytes 3145728 | tf_op jit(solution)/shard_map/reshape | solution.py:294
  76.4 0.1 fusion.15
  76.5 0.7 reshape_reshape.3.place_ref
  77.3 10.4 %shard_map.93 = f32[6144,128]{1,0:T(8,128)} custom-call(s32[1,1536]{1,0:T(1,128)} %reshape_reshape.3.place_ref, bf16[1536,512]{1,0:T(8,128)(2,1)} %reshape.66.arrived_ref), custom_call_target="tpu_custom_call" | custom-call | tf_op jit(solution)/shard_map/pallas_call | solution.py:249
  87.7 3.2 %convert_element_type.34 = bf16[6144,128]{1,0:T(8,128)(2,1)} convert(f32[6144,128]{1,0:T(8,128)} %shard_map.93) | non-fusion elementwise | flops 786432 | bytes 4718592 | tf_op jit(solution)/shard_map/convert_element_type | solution.py:301
  90.9 5.2 %all-to-all-start.1 = ((bf16[256,6,4,128]{3,2,1,0:T(4,128)(2,1)}), bf16[256,6,4,128]{3,2,1,0:T(4,128)(2,1)S(1)}, u32[]{:S(2)}, u32[]{:S(2)}) async-start(bf16[256,6,4,128]{3,2,1,0:T(4,128)(2,1)} %bitcast.14), calls=%async_computation.1 | async-start | bytes 3145728 | tf_op jit(solution)/shard_map/all_to_all | solution.py:304
  96.0 0.1 copy.16
  96.2 0.1 eq.63
  96.3 42.8 %all-to-all-done.1 = bf16[256,6,4,128]{3,2,1,0:T(4,128)(2,1)S(1)} async-done(((bf16[256,6,4,128]{3,2,1,0:T(4,128)(2,1)}), bf16[256,6,4,128]{3,2,1,0:T(4,128)(2,1)S(1)}, u32[]{:S(2)}, u32[]{:S(2)}) %all-to-all-start.1) | async-done | bytes 1572896 | tf_op jit(solution)/shard_map/all_to_all | solution.py:304
  139.1 1.8 %fusion.5 = bf16[1024,512]{1,0:T(8,128)(2,1)S(1)} fusion(bf16[192,8,4,128]{3,2,1,0:T(4,128)(2,1)S(1)} %bitcast.40, s32[1024]{0:T(1024)S(1)} %eq.63), kind=kOutput, calls=%fused_computation.10 | convolution fusion | flops 1612709888 | bytes 2625536 | tf_op jit(solution)/shard_map/dot_general | solution.py:311
  140.9 1.1 fusion.20
  (7 shorter events, 0.1 us)
Async XLA Ops:
  0.6 4.6 %copy-start = (bf16[256,4,128]{2,1,0:T(4,128)(2,1)S(1)}, bf16[256,4,128]{2,1,0:T(4,128)(2,1)}, u32[]{:S(2)}) copy-start(bf16[256,4,128]{2,1,0:T(4,128)(2,1)} %param.9) | copy-start | bytes 786436
  0.6 4.6 %copy-start.1 = (bf16[256,4,128]{2,1,0:T(4,128)(2,1)S(1)}, bf16[256,4,128]{2,1,0:T(4,128)(2,1)}, u32[]{:S(2)}) copy-start(bf16[256,4,128]{2,1,0:T(4,128)(2,1)} %param.8) | copy-start | bytes 786436
  0.7 4.6 %copy-start.2 = (bf16[256,4,128]{2,1,0:T(4,128)(2,1)S(1)}, bf16[256,4,128]{2,1,0:T(4,128)(2,1)}, u32[]{:S(2)}) copy-start(bf16[256,4,128]{2,1,0:T(4,128)(2,1)} %param.7) | copy-start | bytes 786436
  0.7 4.6 %copy-start.3 = (bf16[256,4,128]{2,1,0:T(4,128)(2,1)S(1)}, bf16[256,4,128]{2,1,0:T(4,128)(2,1)}, u32[]{:S(2)}) copy-start(bf16[256,4,128]{2,1,0:T(4,128)(2,1)} %param.6) | copy-start | bytes 786436
  90.9 48.2 %all-to-all-start.1 = ((bf16[256,6,4,128]{3,2,1,0:T(4,128)(2,1)}), bf16[256,6,4,128]{3,2,1,0:T(4,128)(2,1)S(1)}, u32[]{:S(2)}, u32[]{:S(2)}) async-start(bf16[256,6,4,128]{3,2,1,0:T(4,128)(2,1)} %bitcast.14), calls=%async_computation.1 | async-start | bytes 3145728 | tf_op jit(solution)/shard_map/all_to_all | solution.py:304
